TPU v7x, 32 devices: a whole 2x2x4 slice. The times are simulated.
32 devices in a mesh: member: 2 (over y), lon: 4 (over z), lev: 4 (over x, core).
Axes of the slice: x: 2, y: 2, z: 4, core: 2. Of those that a mesh axis runs over, the one named last changes fastest.
Arguments:
- latent: bfloat16 [512, 8, 512], P('lev', 'member', 'lon'), parts along dimension 1, may hold values from -9 to 9
- att_gain: float32 [512], replicated, may hold values from 0.1 to 1.9
- qkv_weight: bfloat16 [3, 512, 512], P(None, 'lev'), may hold values from -0.25 to 0.25
- out_weight: bfloat16 [512, 512], P('lev'), may hold values from -0.25 to 0.25
- stencil_weight: float32 [2, 9, 512], P(None, None, 'lev'), may hold values from -2.5 to 2.5
- block_gain: float32 [2, 512], replicated, may hold values from 0.1 to 1.9
- up_weight: bfloat16 [2, 2048, 512], P(None, 'lev'), may hold values from -0.25 to 0.25
- down_weight: bfloat16 [2, 2048, 512], P(None, 'lev'), may hold values from -0.125 to 0.125
Outputs:
- decoded: bfloat16 [512, 8, 512], P('lev', 'member', 'lon'), parts along dimension 1
There are 2 independent parts, one for each index of `member`. A program takes and returns all parts, laid end to end along the dimension named above; an argument that names none is the same for every part. Nothing has to cross between parts.
All inputs are finite; a program needn't handle non-finite values.
Results may differ from a plain program's by a relative error of at most 0.017.
Values may be sent and summed in bfloat16 or wider, within the bound.
No kernel may reach another device: no remote copies, remote signals or barrier semaphores. Data moves between devices by JAX's collectives and lax.ppermute only.
A program may use at most 64 MiB of HBM per device.

v0:
```python
import math
import jax
import jax.numpy as jnp
from jax import lax
from jax.sharding import PartitionSpec as P

C = 512
H = 8
BLOCKS = 2
attention_scale = 24.0
band_start = 30.0
grid_step = 0.25
epsilon = 1e-06


def secant_rows(count):
    rows = jnp.arange(count).astype(jnp.float32)
    return 1.0 / jnp.cos((band_start + grid_step * rows) * (math.pi / 180.0))


def norm_channels(values, gain):
    scale = lax.rsqrt(jnp.mean(values * values, axis=0, keepdims=True) + epsilon)
    return values * scale * gain[:, None, None]


def unit_heads(values):
    return values * lax.rsqrt(jnp.sum(values * values, axis=1, keepdims=True) + epsilon)


def gather_channels(values):
    return lax.all_gather(values, "lev", axis=0, tiled=True)


def scatter_sum(partial, axis, halo=False):
    devices = lax.axis_size(axis)
    me = lax.axis_index(axis)
    strips = lax.axis_size("lon")
    blocks = partial.reshape(devices, -1, *partial.shape[1:])
    total = jnp.take(blocks, me, axis=0).astype(jnp.float32)
    before = jnp.zeros(total.shape[:-1] + (1,), jnp.float32)
    after = jnp.zeros(total.shape[:-1] + (1,), jnp.float32)
    for shift in range(devices):
        chunk = jnp.take(blocks, (me + shift) % devices, axis=0)
        if shift:
            pairs = [(i, (i + shift) % devices) for i in range(devices)]
            total = total + lax.ppermute(chunk, axis, pairs).astype(jnp.float32)
        if halo:
            for step, edge, sums in ((1, chunk[..., -1:], "before"), (-1, chunk[..., :1], "after")):
                pairs = [
                    (s * devices + i, (s + step) % strips * devices + (i + shift) % devices)
                    for s in range(strips)
                    for i in range(devices)
                ]
                got = lax.ppermute(edge, ("lon", axis), pairs).astype(jnp.float32)
                if sums == "before":
                    before = before + got
                else:
                    after = after + got
    return (total, before, after)


def spread_sum(weight, activation, shape, halo=False):
    partial = lax.dot_general(
        weight, activation, (((0,), (0,)), ((), ())), preferred_element_type=jnp.float32
    ).astype(jnp.bfloat16)
    return scatter_sum(partial.reshape(weight.shape[1], *shape), "lev", halo)


def add_update(state, sums):
    return tuple(((s.astype(jnp.float32) + u).astype(jnp.bfloat16) for s, u in zip(state, sums)))


def gather_strips(values, axis):
    devices = lax.axis_size(axis)
    pieces = [values]
    for shift in range(1, devices):
        pairs = [(i, (i + shift) % devices) for i in range(devices)]
        pieces.append(lax.ppermute(values, axis, pairs))
    return jnp.concatenate(pieces, axis=-1)


def make_fold(queries, pieces):
    key_part, value_part = pieces
    scores = (
        jnp.einsum("hdri,hdrj->hrij", queries, key_part, preferred_element_type=jnp.float32)
        * attention_scale
    )
    weights = jnp.exp(scores)
    numerator = jnp.einsum(
        "hrij,hdrj->hdri",
        weights.astype(jnp.bfloat16),
        value_part,
        preferred_element_type=jnp.float32,
    )
    return (numerator, jnp.sum(weights, axis=3))


def block_apply(state, block_index, stencil_weight, block_gain, up_weight, down_weight, halo):
    extended = jnp.concatenate([state[1], state[0], state[2]], axis=2)
    lat_rows = extended.shape[1]
    out_cols = extended.shape[2] - 2
    secants = secant_rows(lat_rows)[None, :, None]
    padded = jnp.pad(extended.astype(jnp.float32), ((0, 0), (1, 1), (0, 0)))
    tap_weights = stencil_weight[block_index]
    stencil_sum = jnp.zeros((extended.shape[0], lat_rows, out_cols), jnp.float32)
    for row_step in (-1, 0, 1):
        for col_step in (-1, 0, 1):
            shifted = padded[
                :, 1 + row_step : 1 + row_step + lat_rows, 1 + col_step : 1 + col_step + out_cols
            ]
            tap_row = tap_weights[3 * (row_step + 1) + col_step + 1][:, None, None]
            if col_step != 0:
                stencil_sum = stencil_sum + tap_row * secants * shifted
            else:
                stencil_sum = stencil_sum + tap_row * shifted
    smoothed = stencil_sum.astype(jnp.bfloat16)
    full_channels = gather_channels(smoothed)
    block_normed = norm_channels(full_channels.astype(jnp.float32), block_gain[block_index]).astype(
        jnp.bfloat16
    )
    block_normed = block_normed.reshape(full_channels.shape[0], -1)
    hidden = jax.nn.gelu(
        jnp.dot(up_weight[block_index], block_normed, preferred_element_type=jnp.float32)
    ).astype(jnp.bfloat16)
    sums = spread_sum(down_weight[block_index], hidden, state[0].shape[1:], halo)
    return add_update(state, sums)


def per_device(
    latent, att_gain, qkv_weight, out_weight, stencil_weight, block_gain, up_weight, down_weight
):
    ch_local, lat_rows, columns = latent.shape
    head_size = C // H
    heads_local = qkv_weight.shape[1] // head_size
    gathered = gather_channels(latent)
    normed = norm_channels(gathered.astype(jnp.float32), att_gain).astype(jnp.bfloat16)
    projected = jnp.einsum("koc,crw->korw", qkv_weight, normed, preferred_element_type=jnp.float32)
    projected = projected.reshape(3, heads_local, head_size, lat_rows, columns)
    queries = unit_heads(projected[0]).astype(jnp.bfloat16)
    key_rows = unit_heads(projected[1]).astype(jnp.bfloat16)
    value_rows = projected[2].astype(jnp.bfloat16)
    key_value = gather_strips(jnp.stack([key_rows, value_rows]), "lon")
    numerator, denominator = make_fold(queries, (key_value[0], key_value[1]))
    attended = (numerator / denominator[:, None]).astype(jnp.bfloat16)
    strips = lax.axis_size("lon")
    latent_before = lax.ppermute(
        latent[..., -1:], "lon", [(i, (i + 1) % strips) for i in range(strips)]
    )
    latent_after = lax.ppermute(
        latent[..., :1], "lon", [(i, (i - 1) % strips) for i in range(strips)]
    )
    sums = spread_sum(out_weight, attended.reshape(ch_local, -1), latent.shape[1:], True)
    current = add_update((latent, latent_before, latent_after), sums)
    for block_index in range(BLOCKS):
        current = block_apply(
            current,
            block_index,
            stencil_weight,
            block_gain,
            up_weight,
            down_weight,
            block_index < BLOCKS - 1,
        )
    return current[0]


def solution(mesh):
    placed = (
        P("lev", "member", "lon"),
        P(),
        P(None, "lev", None),
        P("lev", None),
        P(None, None, "lev"),
        P(),
        P(None, "lev", None),
        P(None, "lev", None),
    )
    return jax.shard_map(
        per_device, mesh=mesh, in_specs=placed, out_specs=P("lev", "member", "lon"), check_vma=False
    )
```

profile of v0, /device:TPU:0, one launch (start us, length us, event | category | flops | bytes accessed | tf_op | source)
XLA Modules:
  0.0 121.0 jit_solution(17095749814816326519)
XLA Ops:
  0.0 8.9 %all_gather.9 = bf16[512,4,128]{2,1,0:T(4,128)(2,1)S(1)} all-gather(bf16[128,4,128]{2,1,0:T(4,128)(2,1)} %param.10), channel_id=1, replica_groups=mesh['member'=2,'lon'=4,'lev'=4] {'lev'}, dimensions={0}, use_global_device_ids=true | all-gather | bytes 655360 | tf_op jit(solution)/shard_map/all_gather | solution.py:31
  9.0 0.5 fusion.7
  9.5 1.9 %fusion.34 = bf16[512,4,128,1]{2,1,0,3:T(4,128)(2,1)S(1)} fusion(bf16[512,4,128]{2,1,0:T(4,128)(2,1)S(1)} %all_gather.9, f32[512]{0:T(512)} %param.11, f32[4,128]{1,0:T(4,128)S(1)} %add_rsqrt_fusion.4), kind=kLoop, calls=%fused_computation.62 | loop fusion | flops 1048576 | bytes 1052672 | tf_op jit(solution)/shard_map/convert_element_type | solution.py:136
  11.5 0.4 convolution_bitcast_fusion.2
  12.1 3.7 %collective-permute-start.2 = (bf16[2,2,64,4,128]{4,2,3,1,0:T(8,128)(2,1)S(1)}, bf16[2,2,64,4,128]{4,2,3,1,0:T(8,128)(2,1)S(1)}, u32[]{:S(2)}, u32[]{:S(2)}) collective-permute-start(bf16[2,2,64,4,128]{4,2,3,1,0:T(8,128)(2,1)S(1)} %pad_maximum_fusion.1), channel_id=1, source_target_pairs={{0,12},{4,0},{8,4},{12,8},{1,13},{5,1},{9,5},{13,9},{2,14},{6,2},{... | collective-permute-start | bytes 786440 | tf_op jit(solution)/shard_map/ppermute | solution.py:78
  15.8 1.0 collective-permute-start
  16.9 2.9 %collective-permute-start.11 = (bf16[128,4,1]{0,1,2:T(4,128)(2,1)S(1)}, bf16[128,4,1]{0,1,2:T(4,128)(2,1)S(1)}, u32[]{:S(2)}, u32[]{:S(2)}) collective-permute-start(bf16[128,4,1]{0,1,2:T(4,128)(2,1)S(1)} %get-tuple-element.43), channel_id=1, source_target_pairs={{0,12},{4,0},{8,4},{12,8},{1,13},{5,1},{9,5},{13,9},{2,14},{6,2},{... | collective-permute-start | bytes 3080 | tf_op jit(solution)/shard_map/ppermute | solution.py:149
  20.1 2.4 %collective-permute-done.2 = bf16[2,2,64,4,128]{4,2,3,1,0:T(8,128)(2,1)S(1)} collective-permute-done((bf16[2,2,64,4,128]{4,2,3,1,0:T(8,128)(2,1)S(1)}, bf16[2,2,64,4,128]{4,2,3,1,0:T(8,128)(2,1)S(1)}, u32[]{:S(2)}, u32[]{:S(2)}) %collective-permute-start.2) | collective-permute-done | bytes 262176 | tf_op jit(solution)/shard_map/ppermute | solution.py:78
  22.5 16.1 %collective-permute-done.1 = bf16[2,2,64,4,128]{4,2,3,1,0:T(8,128)(2,1)S(1)} collective-permute-done((bf16[2,2,64,4,128]{4,2,3,1,0:T(8,128)(2,1)S(1)}, bf16[2,2,64,4,128]{4,2,3,1,0:T(8,128)(2,1)S(1)}, u32[]{:S(2)}, u32[]{:S(2)}) %collective-permute-start.1) | collective-permute-done | bytes 262176 | tf_op jit(solution)/shard_map/ppermute | solution.py:78
  38.7 0.6 fusion
  39.4 0.5 fusion.6
  40.0 0.3 copy-done.2
  40.3 0.3 fusion.2
  40.7 1.4 %constant_dynamic-slice_fusion.12 = (bf16[1,128,4,128]{1,0,3,2:T(2,128)(2,1)S(1)}, bf16[1,128,4,128]{1,0,3,2:T(2,128)(2,1)S(1)}, bf16[1,128,4,128]{1,0,3,2:T(2,1...) fusion(bf16[4,128,4,128]{1,0,3,2:T(4,128)(2,1)S(1)} %reshape.765, s32[]{:T(128)S(6)} %select_n.83, ...), kind=kLoop, calls=%fused_computation.180 | loop fusion | bytes 1310740 | tf_op jit(solution)/shard_map/jit(_take) | solution.py:39
  42.1 0.2 fusion.109
  42.6 4.1 %collective-permute-start.14 = (bf16[128,4,1]{0,1,2:T(4,128)(2,1)S(1)}, bf16[128,4,1]{0,1,2:T(4,128)(2,1)S(1)}, u32[]{:S(2)}, u32[]{:S(2)}) collective-permute-start(bf16[128,4,1]{0,1,2:T(4,128)(2,1)S(1)} %get-tuple-element.49), channel_id=1, source_target_pairs={{0,14},{1,15},{2,12},{3,13},{4,2},{5,3},{6,0},{7,1},{8,6},{9,7},{1... | collective-permute-start | bytes 3080 | tf_op jit(solution)/shard_map/ppermute | solution.py:54
  47.0 0.2 fusion.108
  47.2 0.9 collective-permute-start.12
  48.1 1.4 %collective-permute-start.6 = (bf16[128,4,1]{0,1,2:T(4,128)(2,1)S(1)}, bf16[128,4,1]{0,1,2:T(4,128)(2,1)S(1)}, u32[]{:S(2)}, u32[]{:S(2)}) collective-permute-start(bf16[128,4,1]{0,1,2:T(4,128)(2,1)S(1)} %get-tuple-element.42), channel_id=1, source_target_pairs={{0,4},{4,8},{8,12},{12,0},{1,5},{5,9},{9,13},{13,1},{2,6},{6,10},{... | collective-permute-start | bytes 3080 | tf_op jit(solution)/shard_map/ppermute | solution.py:146
  49.5 1.9 %collective-permute-start.10 = (bf16[128,4,1]{0,1,2:T(4,128)(2,1)S(1)}, bf16[128,4,1]{0,1,2:T(4,128)(2,1)S(1)}, u32[]{:S(2)}, u32[]{:S(2)}) collective-permute-start(bf16[128,4,1]{0,1,2:T(4,128)(2,1)S(1)} %get-tuple-element.50), channel_id=1, source_target_pairs={{0,7},{1,4},{2,5},{3,6},{4,11},{5,8},{6,9},{7,10},{8,15},{9,12},{1... | collective-permute-start | bytes 3080 | tf_op jit(solution)/shard_map/ppermute | solution.py:54
  51.4 0.9 collective-permute-start.9
  52.3 0.6 collective-permute-start.8
  52.9 1.4 %collective-permute-start.7 = (bf16[128,4,1]{0,1,2:T(4,128)(2,1)S(1)}, bf16[128,4,1]{0,1,2:T(4,128)(2,1)S(1)}, u32[]{:S(2)}, u32[]{:S(2)}) collective-permute-start(bf16[128,4,1]{0,1,2:T(4,128)(2,1)S(1)} %get-tuple-element.44), channel_id=1, source_target_pairs={{0,4},{1,5},{2,6},{3,7},{4,8},{5,9},{6,10},{7,11},{8,12},{9,13},{1... | collective-permute-start | bytes 3080 | tf_op jit(solution)/shard_map/ppermute | solution.py:54
  54.3 2.1 %collective-permute-start.5 = (bf16[128,4,128]{0,1,2:T(4,128)(2,1)S(1)}, bf16[128,4,128]{0,1,2:T(4,128)(2,1)S(1)}, u32[]{:S(2)}, u32[]{:S(2)}) collective-permute-start(bf16[128,4,128]{0,1,2:T(4,128)(2,1)S(1)} %fusion.109), channel_id=1, source_target_pairs={{0,3},{1,0},{2,1},{3,2},{4,7},{5,4},{6,5},{7,6},{8,11},{9,8},{10,9... | collective-permute-start | bytes 393224 | tf_op jit(solution)/shard_map/ppermute | solution.py:46
  56.4 1.1 collective-permute-start.4
  57.7 0.3 collective-permute-done.8
  58.0 0.3 collective-permute-done.7
  58.3 1.9 %collective-permute-done.5 = bf16[128,4,128]{0,1,2:T(4,128)(2,1)S(1)} collective-permute-done((bf16[128,4,128]{0,1,2:T(4,128)(2,1)S(1)}, bf16[128,4,128]{0,1,2:T(4,128)(2,1)S(1)}, u32[]{:S(2)}, u32[]{:S(2)}) %collective-permute-start.5) | collective-permute-done | bytes 131104 | tf_op jit(solution)/shard_map/ppermute | solution.py:46
  60.2 4.0 %collective-permute-done.4 = bf16[128,4,128]{0,1,2:T(4,128)(2,1)S(1)} collective-permute-done((bf16[128,4,128]{0,1,2:T(4,128)(2,1)S(1)}, bf16[128,4,128]{0,1,2:T(4,128)(2,1)S(1)}, u32[]{:S(2)}, u32[]{:S(2)}) %collective-permute-start.4) | collective-permute-done | bytes 131104 | tf_op jit(solution)/shard_map/ppermute | solution.py:46
  64.2 0.3 add_convert_fusion.2
  64.6 0.4 fusion.96
  65.2 6.8 %all_gather.10 = bf16[512,4,128]{2,1,0:T(4,128)(2,1)S(1)} all-gather(bf16[128,4,128]{2,1,0:T(4,128)(2,1)S(1)} %copy.93), channel_id=1, replica_groups=mesh['member'=2,'lon'=4,'lev'=4] {'lev'}, dimensions={0}, use_global_device_ids=true | all-gather | bytes 655360 | tf_op jit(solution)/shard_map/all_gather | solution.py:31
  72.0 0.5 fusion.10
  72.5 1.5 %fusion.12 = bf16[512,4,128]{2,1,0:T(4,128)(2,1)S(1)} fusion(bf16[512,4,128]{2,1,0:T(4,128)(2,1)S(1)} %all_gather.10, f32[512]{0:T(512)S(1)} %bitcast.161, f32[4,128]{1,0:T(4,128)S(1)} %add_rsqrt_fusion.3), kind=kLoop, calls=%fused_computation.28 | loop fusion | flops 1048576 | bytes 1052672 | tf_op jit(solution)/shard_map/convert_element_type | solution.py:118
  74.0 2.0 %fusion.3 = bf16[512,512]{0,1:T(8,128)(2,1)S(1)} fusion(bf16[64,8,4,128]{3,2,1,0:T(4,128)(2,1)S(1)} %bitcast.157, bf16[2,512,512]{2,1,0:T(8,128)(2,1)S(1)} %copy-done.5, bf16[2,512,512]{2,1,0:T(8,128)(2,1)} %param.16), kind=kOutput, calls=%fused_computation.18 | convolution fusion | flops 539492352 | bytes 2097152 | tf_op jit(solution)/shard_map/dot_general | solution.py:63
  76.2 1.5 %constant_dynamic-slice_fusion.5 = (bf16[1,128,4,128]{1,0,3,2:T(2,128)(2,1)S(1)}, bf16[1,128,4,128]{1,0,3,2:T(2,128)(2,1)S(1)}, bf16[1,128,4,128]{1,0,3,2:T(2,12...) fusion(bf16[4,128,4,128]{1,0,3,2:T(4,128)(2,1)S(1)} %reshape.766, s32[]{:T(128)S(6)} %select_n.83, ...), kind=kLoop, calls=%fused_computation.173 | loop fusion | bytes 1310740 | tf_op jit(solution)/shard_map/jit(_take) | solution.py:39
  77.9 2.7 %collective-permute-start.26 = (bf16[128,4,1]{0,1,2:T(4,128)(2,1)S(1)}, bf16[128,4,1]{0,1,2:T(4,128)(2,1)S(1)}, u32[]{:S(2)}, u32[]{:S(2)}) collective-permute-start(bf16[128,4,1]{0,1,2:T(4,128)(2,1)S(1)} %get-tuple-element.41), channel_id=1, source_target_pairs={{0,15},{1,12},{2,13},{3,14},{4,3},{5,0},{6,1},{7,2},{8,7},{9,4},{1... | collective-permute-start | bytes 3080 | tf_op jit(solution)/shard_map/ppermute | solution.py:54
  80.8 1.0 collective-permute-start.25
  82.0 0.7 collective-permute-start.24
  82.9 1.1 collective-permute-start.23
  84.0 1.5 %collective-permute-start.18 = (bf16[128,4,128]{0,1,2:T(4,128)(2,1)S(1)}, bf16[128,4,128]{0,1,2:T(4,128)(2,1)S(1)}, u32[]{:S(2)}, u32[]{:S(2)}) collective-permute-start(bf16[128,4,128]{0,1,2:T(4,128)(2,1)S(1)} %fusion.104), channel_id=1, source_target_pairs={{0,3},{1,0},{2,1},{3,2},{4,7},{5,4},{6,5},{7,6},{8,11},{9,8},{10,9... | collective-permute-start | bytes 393224 | tf_op jit(solution)/shard_map/ppermute | solution.py:46
  85.4 0.9 collective-permute-start.22
  86.3 1.0 collective-permute-start.21
  87.3 1.3 %collective-permute-start.20 = (bf16[128,4,1]{0,1,2:T(4,128)(2,1)S(1)}, bf16[128,4,1]{0,1,2:T(4,128)(2,1)S(1)}, u32[]{:S(2)}, u32[]{:S(2)}) collective-permute-start(bf16[128,4,1]{0,1,2:T(4,128)(2,1)S(1)} %get-tuple-element.36), channel_id=1, source_target_pairs={{0,5},{1,6},{2,7},{3,4},{4,9},{5,10},{6,11},{7,8},{8,13},{9,14},{1... | collective-permute-start | bytes 3080 | tf_op jit(solution)/shard_map/ppermute | solution.py:54
  88.7 1.7 %collective-permute-start.19 = (bf16[128,4,1]{0,1,2:T(4,128)(2,1)S(1)}, bf16[128,4,1]{0,1,2:T(4,128)(2,1)S(1)}, u32[]{:S(2)}, u32[]{:S(2)}) collective-permute-start(bf16[128,4,1]{0,1,2:T(4,128)(2,1)S(1)} %get-tuple-element.34), channel_id=1, source_target_pairs={{0,4},{1,5},{2,6},{3,7},{4,8},{5,9},{6,10},{7,11},{8,12},{9,13},{1... | collective-permute-start | bytes 3080 | tf_op jit(solution)/shard_map/ppermute | solution.py:54
  90.4 1.0 collective-permute-start.17
  91.4 1.2 collective-permute-done.21
  92.6 0.4 collective-permute-done.20
  93.0 1.0 collective-permute-done.19
  94.1 2.4 %collective-permute-done.17 = bf16[128,4,128]{0,1,2:T(4,128)(2,1)S(1)} collective-permute-done((bf16[128,4,128]{0,1,2:T(4,128)(2,1)S(1)}, bf16[128,4,128]{0,1,2:T(4,128)(2,1)S(1)}, u32[]{:S(2)}, u32[]{:S(2)}) %collective-permute-start.17) | collective-permute-done | bytes 131104 | tf_op jit(solution)/shard_map/ppermute | solution.py:46
  96.5 1.0 collective-permute-done.16
  97.5 0.3 add_convert_fusion.1
  97.9 0.4 fusion.95
  98.4 6.8 %all_gather.11 = bf16[512,4,128]{2,1,0:T(4,128)(2,1)S(1)} all-gather(bf16[128,4,128]{2,1,0:T(4,128)(2,1)S(1)} %copy.100), channel_id=1, replica_groups=mesh['member'=2,'lon'=4,'lev'=4] {'lev'}, dimensions={0}, use_global_device_ids=true | all-gather | bytes 655360 | tf_op jit(solution)/shard_map/all_gather | solution.py:31
  105.2 0.5 fusion.13
  105.8 1.5 %fusion.15 = bf16[512,4,128]{2,1,0:T(4,128)(2,1)S(1)} fusion(bf16[512,4,128]{2,1,0:T(4,128)(2,1)S(1)} %all_gather.11, f32[512]{0:T(512)S(1)} %bitcast.160, f32[4,128]{1,0:T(4,128)S(1)} %add_rsqrt_fusion.2), kind=kLoop, calls=%fused_computation.31 | loop fusion | flops 1048576 | bytes 1052672 | tf_op jit(solution)/shard_map/convert_element_type | solution.py:118
  107.3 2.0 %fusion.4 = bf16[512,512]{0,1:T(8,128)(2,1)S(1)} fusion(bf16[64,8,4,128]{3,2,1,0:T(4,128)(2,1)S(1)} %bitcast.158, bf16[2,512,512]{2,1,0:T(8,128)(2,1)S(1)} %copy-done.5, bf16[2,512,512]{2,1,0:T(8,128)(2,1)} %param.16), kind=kOutput, calls=%fused_computation.19 | convolution fusion | flops 539492352 | bytes 2097152 | tf_op jit(solution)/shard_map/dot_general | solution.py:63
  109.4 1.2 %constant_dynamic-slice_fusion.13 = (bf16[1,128,4,128]{1,0,3,2:T(2,128)(2,1)S(1)}, bf16[1,128,4,128]{1,0,3,2:T(2,128)(2,1)S(1)}, bf16[1,128,4,128]{1,0,3,2:T(2,128)(2,1)S(1)}, bf16[1,128,4,128]{1,0,3,2:T(2,128)(2,1)S(1)}) fusion(bf16[4,128,4,128]{1,0,3,2:T(4,128)(2,1)S(1)} %reshape.767, s32[]{:T(128)S(6)} %select_n.83, s32[]{:T(128)S(6)} %select_n.87, ...), kind=kLoop, calls=%fused_computation.181 | loop fusion | bytes 1048592 | tf_op jit(solution)/shard_map/jit(_take) | solution.py:39
  110.8 0.9 collective-permute-start.29
  112.0 1.2 collective-permute-start.28
  113.4 2.3 %collective-permute-done.29 = bf16[128,4,128]{0,1,2:T(4,128)(2,1)S(1)} collective-permute-done((bf16[128,4,128]{0,1,2:T(4,128)(2,1)S(1)}, bf16[128,4,128]{0,1,2:T(4,128)(2,1)S(1)}, u32[]{:S(2)}, u32[]{:S(2)}) %collective-permute-start.29) | collective-permute-done | bytes 131104 | tf_op jit(solution)/shard_map/ppermute | solution.py:46
  115.7 4.2 %collective-permute-done.28 = bf16[128,4,128]{0,1,2:T(4,128)(2,1)S(1)} collective-permute-done((bf16[128,4,128]{0,1,2:T(4,128)(2,1)S(1)}, bf16[128,4,128]{0,1,2:T(4,128)(2,1)S(1)}, u32[]{:S(2)}, u32[]{:S(2)}) %collective-permute-start.28) | collective-permute-done | bytes 131104 | tf_op jit(solution)/shard_map/ppermute | solution.py:46
  119.9 0.3 add_convert_fusion
  120.2 0.8 copy.106
  (82 shorter events, 3.8 us)
Async XLA Ops:
  0.0 11.5 %copy-start = (bf16[3,128,512]{2,1,0:T(8,128)(2,1)S(1)}, bf16[3,128,512]{2,1,0:T(8,128)(2,1)}, u32[]{:S(2)}) copy-start(bf16[3,128,512]{2,1,0:T(8,128)(2,1)} %param.12) | copy-start | bytes 1179652
  11.5 5.3 %copy-start.1 = (bf16[128,4,128]{2,1,0:T(4,128)(2,1)S(1)}, bf16[128,4,128]{2,1,0:T(4,128)(2,1)}, u32[]{:S(2)}) copy-start(bf16[128,4,128]{2,1,0:T(4,128)(2,1)} %param.10) | copy-start | bytes 393220
  11.5 8.4 %copy-start.3 = (f32[2,9,128]{2,0,1:T(2,128)S(1)}, f32[2,9,128]{2,0,1:T(2,128)}, u32[]{:S(2)}) copy-start(f32[2,9,128]{2,0,1:T(2,128)} %param.14) | copy-start | bytes 27652
  12.1 10.4 %collective-permute-start.2 = (bf16[2,2,64,4,128]{4,2,3,1,0:T(8,128)(2,1)S(1)}, bf16[2,2,64,4,128]{4,2,3,1,0:T(8,128)(2,1)S(1)}, u32[]{:S(2)}, u32[]{:S(2)}) collective-permute-start(bf16[2,2,64,4,128]{4,2,3,1,0:T(8,128)(2,1)S(1)} %pad_maximum_fusion.1), channel_id=1, source_target_pairs={{0,12},{4,0},{8,4},{12,8},{1,13},{5,1},{9,5},{13,9},{2,14},{6,2},{... | collective-permute-start | bytes 786440 | tf_op jit(solution)/shard_map/ppermute | solution.py:78
  15.8 22.8 %collective-permute-start.1 = (bf16[2,2,64,4,128]{4,2,3,1,0:T(8,128)(2,1)S(1)}, bf16[2,2,64,4,128]{4,2,3,1,0:T(8,128)(2,1)S(1)}, u32[]{:S(2)}, u32[]{:S(2)}) collective-permute-start(bf16[2,2,64,4,128]{4,2,3,1,0:T(8,128)(2,1)S(1)} %pad_maximum_fusion.1), channel_id=1, source_target_pairs={{0,8},{4,12},{8,0},{12,4},{1,9},{5,13},{9,1},{13,5},{2,10},{6,14},... | collective-permute-start | bytes 786440 | tf_op jit(solution)/shard_map/ppermute | solution.py:78
  15.8 22.8 %collective-permute-start = (bf16[2,2,64,4,128]{4,2,3,1,0:T(8,128)(2,1)S(1)}, bf16[2,2,64,4,128]{4,2,3,1,0:T(8,128)(2,1)S(1)}, u32[]{:S(2)}, u32[]{:S(2)}) collective-permute-start(bf16[2,2,64,4,128]{4,2,3,1,0:T(8,128)(2,1)S(1)} %pad_maximum_fusion.1), channel_id=1, source_target_pairs={{0,4},{4,8},{8,12},{12,0},{1,5},{5,9},{9,13},{13,1},{2,6},{6,10},{... | collective-permute-start | bytes 786440 | tf_op jit(solution)/shard_map/ppermute | solution.py:78
  16.9 31.1 %collective-permute-start.11 = (bf16[128,4,1]{0,1,2:T(4,128)(2,1)S(1)}, bf16[128,4,1]{0,1,2:T(4,128)(2,1)S(1)}, u32[]{:S(2)}, u32[]{:S(2)}) collective-permute-start(bf16[128,4,1]{0,1,2:T(4,128)(2,1)S(1)} %get-tuple-element.43), channel_id=1, source_target_pairs={{0,12},{4,0},{8,4},{12,8},{1,13},{5,1},{9,5},{13,9},{2,14},{6,2},{... | collective-permute-start | bytes 3080 | tf_op jit(solution)/shard_map/ppermute | solution.py:149
  39.3 0.9 copy-start.2
  40.7 7.4 %copy-start.4 = (f32[2,512]{1,0:T(2,128)S(1)}, f32[2,512]{1,0:T(2,128)}, u32[]{:S(2)}) copy-start(f32[2,512]{1,0:T(2,128)} %param.15) | copy-start | bytes 12292
  42.3 7.2 %collective-permute-start.15 = (bf16[128,4,1]{0,1,2:T(4,128)(2,1)S(1)}, bf16[128,4,1]{0,1,2:T(4,128)(2,1)S(1)}, u32[]{:S(2)}, u32[]{:S(2)}) collective-permute-start(bf16[128,4,1]{0,1,2:T(4,128)(2,1)S(1)} %get-tuple-element.51), channel_id=1, source_target_pairs={{0,15},{1,12},{2,13},{3,14},{4,3},{5,0},{6,1},{7,2},{8,7},{9,4},{1... | collective-permute-start | bytes 3080 | tf_op jit(solution)/shard_map/ppermute | solution.py:54
  42.6 8.8 %collective-permute-start.14 = (bf16[128,4,1]{0,1,2:T(4,128)(2,1)S(1)}, bf16[128,4,1]{0,1,2:T(4,128)(2,1)S(1)}, u32[]{:S(2)}, u32[]{:S(2)}) collective-permute-start(bf16[128,4,1]{0,1,2:T(4,128)(2,1)S(1)} %get-tuple-element.49), channel_id=1, source_target_pairs={{0,14},{1,15},{2,12},{3,13},{4,2},{5,3},{6,0},{7,1},{8,6},{9,7},{1... | collective-permute-start | bytes 3080 | tf_op jit(solution)/shard_map/ppermute | solution.py:54
  46.9 5.4 %collective-permute-start.13 = (bf16[128,4,1]{0,1,2:T(4,128)(2,1)S(1)}, bf16[128,4,1]{0,1,2:T(4,128)(2,1)S(1)}, u32[]{:S(2)}, u32[]{:S(2)}) collective-permute-start(bf16[128,4,1]{0,1,2:T(4,128)(2,1)S(1)} %get-tuple-element.47), channel_id=1, source_target_pairs={{0,13},{1,14},{2,15},{3,12},{4,1},{5,2},{6,3},{7,0},{8,5},{9,6},{1... | collective-permute-start | bytes 3080 | tf_op jit(solution)/shard_map/ppermute | solution.py:54
  47.2 5.7 %collective-permute-start.12 = (bf16[128,4,1]{0,1,2:T(4,128)(2,1)S(1)}, bf16[128,4,1]{0,1,2:T(4,128)(2,1)S(1)}, u32[]{:S(2)}, u32[]{:S(2)}) collective-permute-start(bf16[128,4,1]{0,1,2:T(4,128)(2,1)S(1)} %get-tuple-element.45), channel_id=1, source_target_pairs={{0,12},{1,13},{2,14},{3,15},{4,0},{5,1},{6,2},{7,3},{8,4},{9,5},{1... | collective-permute-start | bytes 3080 | tf_op jit(solution)/shard_map/ppermute | solution.py:54
  48.1 6.2 %collective-permute-start.6 = (bf16[128,4,1]{0,1,2:T(4,128)(2,1)S(1)}, bf16[128,4,1]{0,1,2:T(4,128)(2,1)S(1)}, u32[]{:S(2)}, u32[]{:S(2)}) collective-permute-start(bf16[128,4,1]{0,1,2:T(4,128)(2,1)S(1)} %get-tuple-element.42), channel_id=1, source_target_pairs={{0,4},{4,8},{8,12},{12,0},{1,5},{5,9},{9,13},{13,1},{2,6},{6,10},{... | collective-permute-start | bytes 3080 | tf_op jit(solution)/shard_map/ppermute | solution.py:146
  49.5 6.9 %collective-permute-start.10 = (bf16[128,4,1]{0,1,2:T(4,128)(2,1)S(1)}, bf16[128,4,1]{0,1,2:T(4,128)(2,1)S(1)}, u32[]{:S(2)}, u32[]{:S(2)}) collective-permute-start(bf16[128,4,1]{0,1,2:T(4,128)(2,1)S(1)} %get-tuple-element.50), channel_id=1, source_target_pairs={{0,7},{1,4},{2,5},{3,6},{4,11},{5,8},{6,9},{7,10},{8,15},{9,12},{1... | collective-permute-start | bytes 3080 | tf_op jit(solution)/shard_map/ppermute | solution.py:54
  51.4 6.3 %collective-permute-start.9 = (bf16[128,4,1]{0,1,2:T(4,128)(2,1)S(1)}, bf16[128,4,1]{0,1,2:T(4,128)(2,1)S(1)}, u32[]{:S(2)}, u32[]{:S(2)}) collective-permute-start(bf16[128,4,1]{0,1,2:T(4,128)(2,1)S(1)} %get-tuple-element.48), channel_id=1, source_target_pairs={{0,6},{1,7},{2,4},{3,5},{4,10},{5,11},{6,8},{7,9},{8,14},{9,15},{1... | collective-permute-start | bytes 3080 | tf_op jit(solution)/shard_map/ppermute | solution.py:54
  52.3 5.7 %collective-permute-start.8 = (bf16[128,4,1]{0,1,2:T(4,128)(2,1)S(1)}, bf16[128,4,1]{0,1,2:T(4,128)(2,1)S(1)}, u32[]{:S(2)}, u32[]{:S(2)}) collective-permute-start(bf16[128,4,1]{0,1,2:T(4,128)(2,1)S(1)} %get-tuple-element.46), channel_id=1, source_target_pairs={{0,5},{1,6},{2,7},{3,4},{4,9},{5,10},{6,11},{7,8},{8,13},{9,14},{1... | collective-permute-start | bytes 3080 | tf_op jit(solution)/shard_map/ppermute | solution.py:54
  52.9 5.4 %collective-permute-start.7 = (bf16[128,4,1]{0,1,2:T(4,128)(2,1)S(1)}, bf16[128,4,1]{0,1,2:T(4,128)(2,1)S(1)}, u32[]{:S(2)}, u32[]{:S(2)}) collective-permute-start(bf16[128,4,1]{0,1,2:T(4,128)(2,1)S(1)} %get-tuple-element.44), channel_id=1, source_target_pairs={{0,4},{1,5},{2,6},{3,7},{4,8},{5,9},{6,10},{7,11},{8,12},{9,13},{1... | collective-permute-start | bytes 3080 | tf_op jit(solution)/shard_map/ppermute | solution.py:54
  54.3 5.9 %collective-permute-start.5 = (bf16[128,4,128]{0,1,2:T(4,128)(2,1)S(1)}, bf16[128,4,128]{0,1,2:T(4,128)(2,1)S(1)}, u32[]{:S(2)}, u32[]{:S(2)}) collective-permute-start(bf16[128,4,128]{0,1,2:T(4,128)(2,1)S(1)} %fusion.109), channel_id=1, source_target_pairs={{0,3},{1,0},{2,1},{3,2},{4,7},{5,4},{6,5},{7,6},{8,11},{9,8},{10,9... | collective-permute-start | bytes 393224 | tf_op jit(solution)/shard_map/ppermute | solution.py:46
  56.4 7.8 %collective-permute-start.4 = (bf16[128,4,128]{0,1,2:T(4,128)(2,1)S(1)}, bf16[128,4,128]{0,1,2:T(4,128)(2,1)S(1)}, u32[]{:S(2)}, u32[]{:S(2)}) collective-permute-start(bf16[128,4,128]{0,1,2:T(4,128)(2,1)S(1)} %fusion.110), channel_id=1, source_target_pairs={{0,2},{1,3},{2,0},{3,1},{4,6},{5,7},{6,4},{7,5},{8,10},{9,11},{10,... | collective-permute-start | bytes 393224 | tf_op jit(solution)/shard_map/ppermute | solution.py:46
  57.7 6.5 %collective-permute-start.3 = (bf16[128,4,128]{0,1,2:T(4,128)(2,1)S(1)}, bf16[128,4,128]{0,1,2:T(4,128)(2,1)S(1)}, u32[]{:S(2)}, u32[]{:S(2)}) collective-permute-start(bf16[128,4,128]{0,1,2:T(4,128)(2,1)S(1)} %fusion.111), channel_id=1, source_target_pairs={{0,1},{1,2},{2,3},{3,0},{4,5},{5,6},{6,7},{7,4},{8,9},{9,10},{10,1... | collective-permute-start | bytes 393224 | tf_op jit(solution)/shard_map/ppermute | solution.py:46
  64.5 9.6 %copy-start.5 = (bf16[2,512,512]{2,1,0:T(8,128)(2,1)S(1)}, bf16[2,512,512]{2,1,0:T(8,128)(2,1)}, u32[]{:S(2)}) copy-start(bf16[2,512,512]{2,1,0:T(8,128)(2,1)} %param.17) | copy-start | bytes 3145732
  77.9 7.5 %collective-permute-start.26 = (bf16[128,4,1]{0,1,2:T(4,128)(2,1)S(1)}, bf16[128,4,1]{0,1,2:T(4,128)(2,1)S(1)}, u32[]{:S(2)}, u32[]{:S(2)}) collective-permute-start(bf16[128,4,1]{0,1,2:T(4,128)(2,1)S(1)} %get-tuple-element.41), channel_id=1, source_target_pairs={{0,15},{1,12},{2,13},{3,14},{4,3},{5,0},{6,1},{7,2},{8,7},{9,4},{1... | collective-permute-start | bytes 3080 | tf_op jit(solution)/shard_map/ppermute | solution.py:54
  80.8 5.5 %collective-permute-start.25 = (bf16[128,4,1]{0,1,2:T(4,128)(2,1)S(1)}, bf16[128,4,1]{0,1,2:T(4,128)(2,1)S(1)}, u32[]{:S(2)}, u32[]{:S(2)}) collective-permute-start(bf16[128,4,1]{0,1,2:T(4,128)(2,1)S(1)} %get-tuple-element.39), channel_id=1, source_target_pairs={{0,14},{1,15},{2,12},{3,13},{4,2},{5,3},{6,0},{7,1},{8,6},{9,7},{1... | collective-permute-start | bytes 3080 | tf_op jit(solution)/shard_map/ppermute | solution.py:54
  82.0 5.3 %collective-permute-start.24 = (bf16[128,4,1]{0,1,2:T(4,128)(2,1)S(1)}, bf16[128,4,1]{0,1,2:T(4,128)(2,1)S(1)}, u32[]{:S(2)}, u32[]{:S(2)}) collective-permute-start(bf16[128,4,1]{0,1,2:T(4,128)(2,1)S(1)} %get-tuple-element.37), channel_id=1, source_target_pairs={{0,13},{1,14},{2,15},{3,12},{4,1},{5,2},{6,3},{7,0},{8,5},{9,6},{1... | collective-permute-start | bytes 3080 | tf_op jit(solution)/shard_map/ppermute | solution.py:54
  82.9 5.8 %collective-permute-start.23 = (bf16[128,4,1]{0,1,2:T(4,128)(2,1)S(1)}, bf16[128,4,1]{0,1,2:T(4,128)(2,1)S(1)}, u32[]{:S(2)}, u32[]{:S(2)}) collective-permute-start(bf16[128,4,1]{0,1,2:T(4,128)(2,1)S(1)} %get-tuple-element.35), channel_id=1, source_target_pairs={{0,12},{1,13},{2,14},{3,15},{4,0},{5,1},{6,2},{7,3},{8,4},{9,5},{1... | collective-permute-start | bytes 3080 | tf_op jit(solution)/shard_map/ppermute | solution.py:54
  84.0 10.1 %collective-permute-start.18 = (bf16[128,4,128]{0,1,2:T(4,128)(2,1)S(1)}, bf16[128,4,128]{0,1,2:T(4,128)(2,1)S(1)}, u32[]{:S(2)}, u32[]{:S(2)}) collective-permute-start(bf16[128,4,128]{0,1,2:T(4,128)(2,1)S(1)} %fusion.104), channel_id=1, source_target_pairs={{0,3},{1,0},{2,1},{3,2},{4,7},{5,4},{6,5},{7,6},{8,11},{9,8},{10,9... | collective-permute-start | bytes 393224 | tf_op jit(solution)/shard_map/ppermute | solution.py:46
  85.4 4.9 %collective-permute-start.22 = (bf16[128,4,1]{0,1,2:T(4,128)(2,1)S(1)}, bf16[128,4,1]{0,1,2:T(4,128)(2,1)S(1)}, u32[]{:S(2)}, u32[]{:S(2)}) collective-permute-start(bf16[128,4,1]{0,1,2:T(4,128)(2,1)S(1)} %get-tuple-element.40), channel_id=1, source_target_pairs={{0,7},{1,4},{2,5},{3,6},{4,11},{5,8},{6,9},{7,10},{8,15},{9,12},{1... | collective-permute-start | bytes 3080 | tf_op jit(solution)/shard_map/ppermute | solution.py:54
  86.3 6.3 %collective-permute-start.21 = (bf16[128,4,1]{0,1,2:T(4,128)(2,1)S(1)}, bf16[128,4,1]{0,1,2:T(4,128)(2,1)S(1)}, u32[]{:S(2)}, u32[]{:S(2)}) collective-permute-start(bf16[128,4,1]{0,1,2:T(4,128)(2,1)S(1)} %get-tuple-element.38), channel_id=1, source_target_pairs={{0,6},{1,7},{2,4},{3,5},{4,10},{5,11},{6,8},{7,9},{8,14},{9,15},{1... | collective-permute-start | bytes 3080 | tf_op jit(solution)/shard_map/ppermute | solution.py:54
  87.3 5.7 %collective-permute-start.20 = (bf16[128,4,1]{0,1,2:T(4,128)(2,1)S(1)}, bf16[128,4,1]{0,1,2:T(4,128)(2,1)S(1)}, u32[]{:S(2)}, u32[]{:S(2)}) collective-permute-start(bf16[128,4,1]{0,1,2:T(4,128)(2,1)S(1)} %get-tuple-element.36), channel_id=1, source_target_pairs={{0,5},{1,6},{2,7},{3,4},{4,9},{5,10},{6,11},{7,8},{8,13},{9,14},{1... | collective-permute-start | bytes 3080 | tf_op jit(solution)/shard_map/ppermute | solution.py:54
  88.7 5.4 %collective-permute-start.19 = (bf16[128,4,1]{0,1,2:T(4,128)(2,1)S(1)}, bf16[128,4,1]{0,1,2:T(4,128)(2,1)S(1)}, u32[]{:S(2)}, u32[]{:S(2)}) collective-permute-start(bf16[128,4,1]{0,1,2:T(4,128)(2,1)S(1)} %get-tuple-element.34), channel_id=1, source_target_pairs={{0,4},{1,5},{2,6},{3,7},{4,8},{5,9},{6,10},{7,11},{8,12},{9,13},{1... | collective-permute-start | bytes 3080 | tf_op jit(solution)/shard_map/ppermute | solution.py:54
  90.4 6.1 %collective-permute-start.17 = (bf16[128,4,128]{0,1,2:T(4,128)(2,1)S(1)}, bf16[128,4,128]{0,1,2:T(4,128)(2,1)S(1)}, u32[]{:S(2)}, u32[]{:S(2)}) collective-permute-start(bf16[128,4,128]{0,1,2:T(4,128)(2,1)S(1)} %fusion.105), channel_id=1, source_target_pairs={{0,2},{1,3},{2,0},{3,1},{4,6},{5,7},{6,4},{7,5},{8,10},{9,11},{10,... | collective-permute-start | bytes 393224 | tf_op jit(solution)/shard_map/ppermute | solution.py:46
  92.6 4.9 %collective-permute-start.16 = (bf16[128,4,128]{0,1,2:T(4,128)(2,1)S(1)}, bf16[128,4,128]{0,1,2:T(4,128)(2,1)S(1)}, u32[]{:S(2)}, u32[]{:S(2)}) collective-permute-start(bf16[128,4,128]{0,1,2:T(4,128)(2,1)S(1)} %fusion.106), channel_id=1, source_target_pairs={{0,1},{1,2},{2,3},{3,0},{4,5},{5,6},{6,7},{7,4},{8,9},{9,10},{10,1... | collective-permute-start | bytes 393224 | tf_op jit(solution)/shard_map/ppermute | solution.py:46
  110.8 4.8 %collective-permute-start.29 = (bf16[128,4,128]{0,1,2:T(4,128)(2,1)S(1)}, bf16[128,4,128]{0,1,2:T(4,128)(2,1)S(1)}, u32[]{:S(2)}, u32[]{:S(2)}) collective-permute-start(bf16[128,4,128]{0,1,2:T(4,128)(2,1)S(1)} %fusion.99), channel_id=1, source_target_pairs={{0,3},{1,0},{2,1},{3,2},{4,7},{5,4},{6,5},{7,6},{8,11},{9,8},{10,9... | collective-permute-start | bytes 393224 | tf_op jit(solution)/shard_map/ppermute | solution.py:46
  112.0 7.9 %collective-permute-start.28 = (bf16[128,4,128]{0,1,2:T(4,128)(2,1)S(1)}, bf16[128,4,128]{0,1,2:T(4,128)(2,1)S(1)}, u32[]{:S(2)}, u32[]{:S(2)}) collective-permute-start(bf16[128,4,128]{0,1,2:T(4,128)(2,1)S(1)} %fusion.100), channel_id=1, source_target_pairs={{0,2},{1,3},{2,0},{3,1},{4,6},{5,7},{6,4},{7,5},{8,10},{9,11},{10,... | collective-permute-start | bytes 393224 | tf_op jit(solution)/shard_map/ppermute | solution.py:46
  113.3 6.6 %collective-permute-start.27 = (bf16[128,4,128]{0,1,2:T(4,128)(2,1)S(1)}, bf16[128,4,128]{0,1,2:T(4,128)(2,1)S(1)}, u32[]{:S(2)}, u32[]{:S(2)}) collective-permute-start(bf16[128,4,128]{0,1,2:T(4,128)(2,1)S(1)} %fusion.101), channel_id=1, source_target_pairs={{0,1},{1,2},{2,3},{3,0},{4,5},{5,6},{6,7},{7,4},{8,9},{9,10},{10,1... | collective-permute-start | bytes 393224 | tf_op jit(solution)/shard_map/ppermute | solution.py:46
where the time goes:
time: 121 us
  waiting for transfers between devices  37.7 us (31%)
  starting transfers between devices  37.1 us (31%)
  blocking collectives  22.5 us (19%)
  other arithmetic  11.1 us (9%)
  local copies, waits for them, and re-layouts  6.3 us (5%)
  matrix products  5.77 us (5%)
    all_gather x3, blocking collectives, gather_channels(): return lax.all_gather(values, 'lev', axis=0, tiled=True)  22.5 us
    ppermute x16, starting transfers between devices, scatter_sum(): got = lax.ppermute(edge, ('lon', axis), pairs).astype(jnp.float32)  20.2 us
    ppermute x3, waiting for transfers between devices, gather_strips(): pieces.append(lax.ppermute(values, axis, pairs))  18.5 us
    ppermute x9, waiting for transfers between devices, scatter_sum(): total = total + lax.ppermute(chunk, axis, pairs).astype(jnp.float32)  15.8 us
    ppermute x9, starting transfers between devices, scatter_sum(): total = total + lax.ppermute(chunk, axis, pairs).astype(jnp.float32)  7.84 us
    ppermute x3, starting transfers between devices, gather_strips(): pieces.append(lax.ppermute(values, axis, pairs))  4.67 us
    dot_general x3, matrix products, spread_sum(): lax.dot_general(weight, activation, (((0,), (0,)), ((), ())), preferred_e...  4.29 us
    another operation x3, local copies, waits for them, and re-layouts, scatter_sum(): total = jnp.take(blocks, me, axis=0).astype(jnp.float32)  4.17 us
  transfers between devices with their start and end apart: 30, of which 14 were waited for; matrix products, arithmetic and copies ran while one was open for 4% of the time, Pallas kernels for 0%

commit v1 on v0

--- a/solution.py
+++ b/solution.py
@@ -11,6 +11,18 @@
 band_start = 30.0
 grid_step = 0.25
 epsilon = 1e-06
+
+
+def collect(shard, axis, dim):
+    ways, here, step = (lax.axis_size(axis), lax.axis_index(axis), shard.shape[dim])
+    line, have = (shard, 1)
+    while have < ways:
+        line = jnp.concatenate(
+            [line, lax.ppermute(line, axis, [(d, (d - have) % ways) for d in range(ways)])],
+            axis=dim,
+        )
+        have = 2 * have
+    return jnp.roll(line, here * step, axis=dim)
 
 
 def secant_rows(count):
@@ -28,7 +40,7 @@
 
 
 def gather_channels(values):
-    return lax.all_gather(values, "lev", axis=0, tiled=True)
+    return collect(values, "lev", 0)
 
 
 def scatter_sum(partial, axis, halo=False):

time: 121 us -> 145 us (1.20)
  blocking collectives: 22.5 us -> 0 us
  starting transfers between devices: 37.1 us -> 55.2 us
  waiting for transfers between devices: 37.7 us -> 55.4 us
  other arithmetic: 11.1 us -> 19.3 us
  local copies, waits for them, and re-layouts: 6.3 us -> 8.14 us
    ppermute x0 -> x6, waiting for transfers between devices: none -> 26.8 us  [collect(): lax.ppermute(line, axis, [(d, (d - have) % ways) for d in range(ways)])]
    all_gather x3 -> x0, blocking collectives: 22.5 us -> none  [gather_channels(): return lax.all_gather(values, 'lev', axis=0, tiled=True)]
    ppermute x0 -> x6, starting transfers between devices: none -> 9.21 us  [collect(): lax.ppermute(line, axis, [(d, (d - have) % ways) for d in range(ways)])]
    reduce_sum x3, other arithmetic: 1.65 us -> 10.8 us  [norm_channels(): jnp.mean(values * values, axis=0, keepdims=True) + epsilon]
    ppermute x16, starting transfers between devices: 20.2 us -> 26.7 us  [scatter_sum(): got = lax.ppermute(edge, ('lon', axis), pairs).astype(jnp.float32)]
    ppermute x16, waiting for transfers between devices: 3.41 us -> 0.04 us  [scatter_sum(): got = lax.ppermute(edge, ('lon', axis), pairs).astype(jnp.float32)]
    ppermute x9, waiting for transfers between devices: 15.8 us -> 12.8 us  [scatter_sum(): total = total + lax.ppermute(chunk, axis, pairs).astype(jnp.float32)]
    ppermute x3, waiting for transfers between devices: 18.5 us -> 15.7 us  [gather_strips(): pieces.append(lax.ppermute(values, axis, pairs))]
  transfers between devices with their start and end apart: 30 -> 36, of which waited for: 14 -> 15; matrix products, arithmetic and copies ran while one was open for 4% -> 13% of each run, Pallas kernels for 0% -> 0%
where the time goes in v1:
time: 145 us; the launch traced here: 144 us
  waiting for transfers between devices  55.4 us (38%)
  starting transfers between devices  55.2 us (38%)
  other arithmetic  19.3 us (13%)
  local copies, waits for them, and re-layouts  8.14 us (6%)
  matrix products  5.73 us (4%)
    ppermute x6, waiting for transfers between devices, collect(): lax.ppermute(line, axis, [(d, (d - have) % ways) for d in range(ways)])  26.8 us
    ppermute x16, starting transfers between devices, scatter_sum(): got = lax.ppermute(edge, ('lon', axis), pairs).astype(jnp.float32)  26.7 us
    ppermute x3, waiting for transfers between devices, gather_strips(): pieces.append(lax.ppermute(values, axis, pairs))  15.7 us
    ppermute x9, waiting for transfers between devices, scatter_sum(): total = total + lax.ppermute(chunk, axis, pairs).astype(jnp.float32)  12.8 us
    reduce_sum x3, other arithmetic, norm_channels(): jnp.mean(values * values, axis=0, keepdims=True) + epsilon  10.8 us
    ppermute x6, starting transfers between devices, collect(): lax.ppermute(line, axis, [(d, (d - have) % ways) for d in range(ways)])  9.21 us
    ppermute x9, starting transfers between devices, scatter_sum(): total = total + lax.ppermute(chunk, axis, pairs).astype(jnp.float32)  8.29 us
    ppermute x3, starting transfers between devices, gather_strips(): pieces.append(lax.ppermute(values, axis, pairs))  5.57 us
  transfers between devices with their start and end apart: 36, of which 15 were waited for; matrix products, arithmetic and copies ran while one was open for 13% of the time, Pallas kernels for 0%

profile of v1, /device:TPU:0, one launch (start us, length us, event | category | flops | bytes accessed | tf_op | source)
XLA Modules:
  0.0 144.3 jit_solution(10045885630686537973)
XLA Ops:
  0.0 2.4 %collective-permute-start = (bf16[128,4,128]{2,1,0:T(4,128)(2,1)}, bf16[128,4,128]{2,1,0:T(4,128)(2,1)S(1)}, u32[]{:S(2)}, u32[]{:S(2)}) collective-permute-start(bf16[128,4,128]{2,1,0:T(4,128)(2,1)} %param.12), channel_id=1, source_target_pairs={{0,3},{1,0},{2,1},{3,2},{4,7},{5,4},{6,5},{7,6},{8,11},{9,8},{10,9... | collective-permute-start | bytes 393224 | tf_op jit(solution)/shard_map/ppermute | solution.py:21
  2.4 1.1 copy.138
  3.5 1.6 %collective-permute-start.8 = (bf16[128,4,1]{0,1,2:T(4,128)(2,1)S(1)}, bf16[128,4,1]{0,1,2:T(4,128)(2,1)S(1)}, u32[]{:S(2)}, u32[]{:S(2)}) collective-permute-start(bf16[128,4,1]{0,1,2:T(4,128)(2,1)S(1)} %get-tuple-element.49), channel_id=1, source_target_pairs={{0,4},{4,8},{8,12},{12,0},{1,5},{5,9},{9,13},{13,1},{2,6},{6,10},{... | collective-permute-start | bytes 3080 | tf_op jit(solution)/shard_map/ppermute | solution.py:158
  5.2 1.1 pad_maximum_fusion.1
  6.3 0.6 collective-permute-start.1
  7.1 0.9 slice_bitcast_fusion.12
  7.9 7.3 %collective-permute-done.1 = bf16[256,4,128]{2,1,0:T(4,128)(2,1)S(1)} collective-permute-done((bf16[256,4,128]{2,1,0:T(4,128)(2,1)S(1)}, bf16[256,4,128]{2,1,0:T(4,128)(2,1)S(1)}, u32[]{:S(2)}, u32[]{:S(2)}) %collective-permute-start.1) | collective-permute-done | bytes 262176 | tf_op jit(solution)/shard_map/ppermute | solution.py:21
  15.3 7.3 %fusion.7 = (f32[4,128]{1,0:T(4,128)S(1)}, bf16[512,4,128]{2,1,0:T(4,128)(2,1)S(1)}) fusion(s32[]{:T(128)S(6)} %select_n.97, bf16[256,4,128]{2,1,0:T(4,128)(2,1)S(1)} %collective-permute-done.1, bf16[128,4,128]{2,1,0:T(4,128)(2,1)S(1)} %collective-permute-done, bf16[128,4,128]{2,1,0:T(4,128)(2,1)} %param.12), kind=kLoop, calls=%fused_computation.23 | loop fusion | flops 2096640 | bytes 1050628 | tf_op jit(solution)/shard_map/reduce_sum | solution.py:34
  22.6 1.9 %fusion.49 = bf16[512,4,128,1]{2,1,0,3:T(4,128)(2,1)S(1)} fusion(bf16[512,4,128]{2,1,0:T(4,128)(2,1)S(1)} %get-tuple-element.23, f32[512]{0:T(512)} %param.13, f32[4,128]{1,0:T(4,128)S(1)} %add_rsqrt_fusion.4), kind=kLoop, calls=%fused_computation.95 | loop fusion | flops 1048576 | bytes 1052672 | tf_op jit(solution)/shard_map/convert_element_type | solution.py:148
  24.6 0.4 convolution_bitcast_fusion.2
  25.2 1.6 %collective-permute-start.2 = (bf16[2,2,64,4,128]{4,2,3,1,0:T(8,128)(2,1)S(1)}, bf16[2,2,64,4,128]{4,2,3,1,0:T(8,128)(2,1)S(1)}, u32[]{:S(2)}, u32[]{:S(2)}) collective-permute-start(bf16[2,2,64,4,128]{4,2,3,1,0:T(8,128)(2,1)S(1)} %pad_maximum_fusion.2), channel_id=1, source_target_pairs={{0,4},{4,8},{8,12},{12,0},{1,5},{5,9},{9,13},{13,1},{2,6},{6,10},{... | collective-permute-start | bytes 786440 | tf_op jit(solution)/shard_map/ppermute | solution.py:90
  26.8 2.6 %collective-permute-start.3 = (bf16[2,2,64,4,128]{4,2,3,1,0:T(8,128)(2,1)S(1)}, bf16[2,2,64,4,128]{4,2,3,1,0:T(8,128)(2,1)S(1)}, u32[]{:S(2)}, u32[]{:S(2)}) collective-permute-start(bf16[2,2,64,4,128]{4,2,3,1,0:T(8,128)(2,1)S(1)} %pad_maximum_fusion.2), channel_id=1, source_target_pairs={{0,8},{4,12},{8,0},{12,4},{1,9},{5,13},{9,1},{13,5},{2,10},{6,14},... | collective-permute-start | bytes 786440 | tf_op jit(solution)/shard_map/ppermute | solution.py:90
  29.4 1.3 collective-permute-start.4
  30.8 5.6 %collective-permute-done.2 = bf16[2,2,64,4,128]{4,2,3,1,0:T(8,128)(2,1)S(1)} collective-permute-done((bf16[2,2,64,4,128]{4,2,3,1,0:T(8,128)(2,1)S(1)}, bf16[2,2,64,4,128]{4,2,3,1,0:T(8,128)(2,1)S(1)}, u32[]{:S(2)}, u32[]{:S(2)}) %collective-permute-start.2) | collective-permute-done | bytes 262176 | tf_op jit(solution)/shard_map/ppermute | solution.py:90
  36.4 10.2 %collective-permute-done.3 = bf16[2,2,64,4,128]{4,2,3,1,0:T(8,128)(2,1)S(1)} collective-permute-done((bf16[2,2,64,4,128]{4,2,3,1,0:T(8,128)(2,1)S(1)}, bf16[2,2,64,4,128]{4,2,3,1,0:T(8,128)(2,1)S(1)}, u32[]{:S(2)}, u32[]{:S(2)}) %collective-permute-start.3) | collective-permute-done | bytes 262176 | tf_op jit(solution)/shard_map/ppermute | solution.py:90
  46.7 0.6 fusion
  47.3 0.5 fusion.6
  48.2 0.3 fusion.2
  48.7 1.6 %constant_dynamic-slice_fusion.12 = (bf16[1,128,4,128]{1,0,3,2:T(2,128)(2,1)S(1)}, bf16[1,128,4,128]{1,0,3,2:T(2,128)(2,1)S(1)}, bf16[1,128,4,128]{1,0,3,2:T(2,1...) fusion(bf16[4,128,4,128]{1,0,3,2:T(4,128)(2,1)S(1)} %reshape.765, s32[]{:T(128)S(6)} %select_n.98, ...), kind=kLoop, calls=%fused_computation.212 | loop fusion | bytes 1310740 | tf_op jit(solution)/shard_map/jit(_take) | solution.py:51
  50.4 6.1 %collective-permute-start.9 = (bf16[128,4,1]{0,1,2:T(4,128)(2,1)S(1)}, bf16[128,4,1]{0,1,2:T(4,128)(2,1)S(1)}, u32[]{:S(2)}, u32[]{:S(2)}) collective-permute-start(bf16[128,4,1]{0,1,2:T(4,128)(2,1)S(1)} %get-tuple-element.51), channel_id=1, source_target_pairs={{0,4},{1,5},{2,6},{3,7},{4,8},{5,9},{6,10},{7,11},{8,12},{9,13},{1... | collective-permute-start | bytes 3080 | tf_op jit(solution)/shard_map/ppermute | solution.py:66
  57.1 1.3 collective-permute-start.11
  58.6 1.6 %collective-permute-start.12 = (bf16[128,4,1]{0,1,2:T(4,128)(2,1)S(1)}, bf16[128,4,1]{0,1,2:T(4,128)(2,1)S(1)}, u32[]{:S(2)}, u32[]{:S(2)}) collective-permute-start(bf16[128,4,1]{0,1,2:T(4,128)(2,1)S(1)} %get-tuple-element.57), channel_id=1, source_target_pairs={{0,7},{1,4},{2,5},{3,6},{4,11},{5,8},{6,9},{7,10},{8,15},{9,12},{1... | collective-permute-start | bytes 3080 | tf_op jit(solution)/shard_map/ppermute | solution.py:66
  60.2 3.8 %collective-permute-start.13 = (bf16[128,4,1]{0,1,2:T(4,128)(2,1)S(1)}, bf16[128,4,1]{0,1,2:T(4,128)(2,1)S(1)}, u32[]{:S(2)}, u32[]{:S(2)}) collective-permute-start(bf16[128,4,1]{0,1,2:T(4,128)(2,1)S(1)} %get-tuple-element.50), channel_id=1, source_target_pairs={{0,12},{4,0},{8,4},{12,8},{1,13},{5,1},{9,5},{13,9},{2,14},{6,2},{... | collective-permute-start | bytes 3080 | tf_op jit(solution)/shard_map/ppermute | solution.py:161
  64.1 2.5 %collective-permute-start.16 = (bf16[128,4,1]{0,1,2:T(4,128)(2,1)S(1)}, bf16[128,4,1]{0,1,2:T(4,128)(2,1)S(1)}, u32[]{:S(2)}, u32[]{:S(2)}) collective-permute-start(bf16[128,4,1]{0,1,2:T(4,128)(2,1)S(1)} %get-tuple-element.56), channel_id=1, source_target_pairs={{0,14},{1,15},{2,12},{3,13},{4,2},{5,3},{6,0},{7,1},{8,6},{9,7},{1... | collective-permute-start | bytes 3080 | tf_op jit(solution)/shard_map/ppermute | solution.py:66
  66.6 3.3 %collective-permute-start.17 = (bf16[128,4,1]{0,1,2:T(4,128)(2,1)S(1)}, bf16[128,4,1]{0,1,2:T(4,128)(2,1)S(1)}, u32[]{:S(2)}, u32[]{:S(2)}) collective-permute-start(bf16[128,4,1]{0,1,2:T(4,128)(2,1)S(1)} %get-tuple-element.58), channel_id=1, source_target_pairs={{0,15},{1,12},{2,13},{3,14},{4,3},{5,0},{6,1},{7,2},{8,7},{9,4},{1... | collective-permute-start | bytes 3080 | tf_op jit(solution)/shard_map/ppermute | solution.py:66
  70.0 0.9 collective-permute-start.6
  70.9 1.4 collective-permute-start.7
  72.3 2.9 %collective-permute-done.5 = bf16[128,4,128]{0,1,2:T(4,128)(2,1)S(1)} collective-permute-done((bf16[128,4,128]{0,1,2:T(4,128)(2,1)S(1)}, bf16[128,4,128]{0,1,2:T(4,128)(2,1)S(1)}, u32[]{:S(2)}, u32[]{:S(2)}) %collective-permute-start.5) | collective-permute-done | bytes 131104 | tf_op jit(solution)/shard_map/ppermute | solution.py:58
  75.2 1.2 collective-permute-done.6
  76.4 0.5 collective-permute-done.7
  77.4 0.4 fusion.103
  77.8 2.0 %collective-permute-start.18 = (bf16[128,4,128]{0,1,2:T(4,128)(2,1)S(1)}, bf16[128,4,128]{0,1,2:T(4,128)(2,1)S(1)}, u32[]{:S(2)}, u32[]{:S(2)}) collective-permute-start(bf16[128,4,128]{0,1,2:T(4,128)(2,1)S(1)} %fusion.103), channel_id=1, source_target_pairs={{0,3},{1,0},{2,1},{3,2},{4,7},{5,4},{6,5},{7,6},{8,11},{9,8},{10,9... | collective-permute-start | bytes 393224 | tf_op jit(solution)/shard_map/ppermute | solution.py:21
  79.7 2.5 %collective-permute-done.18 = bf16[128,4,128]{0,1,2:T(4,128)(2,1)S(1)} collective-permute-done((bf16[128,4,128]{0,1,2:T(4,128)(2,1)S(1)}, bf16[128,4,128]{0,1,2:T(4,128)(2,1)S(1)}, u32[]{:S(2)}, u32[]{:S(2)}) %collective-permute-start.18) | collective-permute-done | bytes 131104 | tf_op jit(solution)/shard_map/ppermute | solution.py:21
  82.4 1.3 collective-permute-start.19
  83.7 7.5 %collective-permute-done.19 = bf16[256,4,128]{0,1,2:T(4,128)(2,1)S(1)} collective-permute-done((bf16[256,4,128]{0,1,2:T(4,128)(2,1)S(1)}, bf16[256,4,128]{0,1,2:T(4,128)(2,1)S(1)}, u32[]{:S(2)}, u32[]{:S(2)}) %collective-permute-start.19) | collective-permute-done | bytes 262176 | tf_op jit(solution)/shard_map/ppermute | solution.py:21
  91.2 1.7 %fusion.10 = (f32[4,128]{0,1:T(8,128)S(1)}, bf16[512,4,128]{0,1,2:T(4,128)(2,1)S(1)}) fusion(s32[]{:T(128)S(6)} %select_n.97, bf16[256,4,128]{0,1,2:T(4,128)(2,1)S(1)} %collective-permute-done.19, bf16[128,4,128]{0,1,2:T(4,128)(2,1)S(1)} %collective-permute-done.18, bf16[128,4,128]{0,1,2:T(4,128)(2,1)S(1)} %fusion.103), kind=kLoop, calls=%fused_computation.26 | loop fusion | flops 3931648 | bytes 1050628 | tf_op jit(solution)/shard_map/reduce_sum | solution.py:34
  93.0 0.3 fusion.12
  93.4 2.0 %fusion.3 = bf16[512,512]{0,1:T(8,128)(2,1)S(1)} fusion(bf16[512,512]{0,1:T(8,128)(2,1)S(1)} %bitcast.151, bf16[2,512,512]{2,1,0:T(8,128)(2,1)S(1)} %copy-done.3, bf16[2,512,512]{2,1,0:T(8,128)(2,1)} %param.18), kind=kOutput, calls=%fused_computation.18 | convolution fusion | flops 539492352 | bytes 2097152 | tf_op jit(solution)/shard_map/dot_general | solution.py:75
  95.6 1.6 %constant_dynamic-slice_fusion.1 = (bf16[1,128,4,128]{1,0,3,2:T(2,128)(2,1)S(1)}, bf16[1,128,4,128]{1,0,3,2:T(2,128)(2,1)S(1)}, bf16[1,128,4,128]{1,0,3,2:T(2,12...) fusion(bf16[4,128,4,128]{1,0,3,2:T(4,128)(2,1)S(1)} %reshape.766, s32[]{:T(128)S(6)} %select_n.98, ...), kind=kLoop, calls=%fused_computation.201 | loop fusion | bytes 1310740 | tf_op jit(solution)/shard_map/jit(_take) | solution.py:51
  97.6 0.6 collective-permute-start.24
  98.4 1.5 %collective-permute-start.25 = (bf16[128,4,1]{0,1,2:T(4,128)(2,1)S(1)}, bf16[128,4,1]{0,1,2:T(4,128)(2,1)S(1)}, u32[]{:S(2)}, u32[]{:S(2)}) collective-permute-start(bf16[128,4,1]{0,1,2:T(4,128)(2,1)S(1)} %get-tuple-element.45), channel_id=1, source_target_pairs={{0,6},{1,7},{2,4},{3,5},{4,10},{5,11},{6,8},{7,9},{8,14},{9,15},{1... | collective-permute-start | bytes 3080 | tf_op jit(solution)/shard_map/ppermute | solution.py:66
  100.1 4.3 %collective-permute-start.26 = (bf16[128,4,1]{0,1,2:T(4,128)(2,1)S(1)}, bf16[128,4,1]{0,1,2:T(4,128)(2,1)S(1)}, u32[]{:S(2)}, u32[]{:S(2)}) collective-permute-start(bf16[128,4,1]{0,1,2:T(4,128)(2,1)S(1)} %get-tuple-element.47), channel_id=1, source_target_pairs={{0,7},{1,4},{2,5},{3,6},{4,11},{5,8},{6,9},{7,10},{8,15},{9,12},{1... | collective-permute-start | bytes 3080 | tf_op jit(solution)/shard_map/ppermute | solution.py:66
  104.5 1.7 %collective-permute-start.28 = (bf16[128,4,1]{0,1,2:T(4,128)(2,1)S(1)}, bf16[128,4,1]{0,1,2:T(4,128)(2,1)S(1)}, u32[]{:S(2)}, u32[]{:S(2)}) collective-permute-start(bf16[128,4,1]{0,1,2:T(4,128)(2,1)S(1)} %get-tuple-element.44), channel_id=1, source_target_pairs={{0,13},{1,14},{2,15},{3,12},{4,1},{5,2},{6,3},{7,0},{8,5},{9,6},{1... | collective-permute-start | bytes 3080 | tf_op jit(solution)/shard_map/ppermute | solution.py:66
  106.2 2.0 %collective-permute-start.29 = (bf16[128,4,1]{0,1,2:T(4,128)(2,1)S(1)}, bf16[128,4,1]{0,1,2:T(4,128)(2,1)S(1)}, u32[]{:S(2)}, u32[]{:S(2)}) collective-permute-start(bf16[128,4,1]{0,1,2:T(4,128)(2,1)S(1)} %get-tuple-element.46), channel_id=1, source_target_pairs={{0,14},{1,15},{2,12},{3,13},{4,2},{5,3},{6,0},{7,1},{8,6},{9,7},{1... | collective-permute-start | bytes 3080 | tf_op jit(solution)/shard_map/ppermute | solution.py:66
  108.3 1.3 collective-permute-start.30
  109.6 1.6 %collective-permute-start.21 = (bf16[128,4,128]{0,1,2:T(4,128)(2,1)S(1)}, bf16[128,4,128]{0,1,2:T(4,128)(2,1)S(1)}, u32[]{:S(2)}, u32[]{:S(2)}) collective-permute-start(bf16[128,4,128]{0,1,2:T(4,128)(2,1)S(1)} %fusion.112), channel_id=1, source_target_pairs={{0,2},{1,3},{2,0},{3,1},{4,6},{5,7},{6,4},{7,5},{8,10},{9,11},{10,... | collective-permute-start | bytes 393224 | tf_op jit(solution)/shard_map/ppermute | solution.py:58
  111.3 0.6 collective-permute-start.22
  111.9 4.0 %collective-permute-done.21 = bf16[128,4,128]{0,1,2:T(4,128)(2,1)S(1)} collective-permute-done((bf16[128,4,128]{0,1,2:T(4,128)(2,1)S(1)}, bf16[128,4,128]{0,1,2:T(4,128)(2,1)S(1)}, u32[]{:S(2)}, u32[]{:S(2)}) %collective-permute-start.21) | collective-permute-done | bytes 131104 | tf_op jit(solution)/shard_map/ppermute | solution.py:58
  116.3 0.4 fusion.102
  116.7 1.3 collective-permute-start.31
  118.0 2.5 %collective-permute-done.31 = bf16[128,4,128]{0,1,2:T(4,128)(2,1)S(1)} collective-permute-done((bf16[128,4,128]{0,1,2:T(4,128)(2,1)S(1)}, bf16[128,4,128]{0,1,2:T(4,128)(2,1)S(1)}, u32[]{:S(2)}, u32[]{:S(2)}) %collective-permute-start.31) | collective-permute-done | bytes 131104 | tf_op jit(solution)/shard_map/ppermute | solution.py:21
  120.7 1.6 %collective-permute-start.32 = (bf16[256,4,128]{0,1,2:T(4,128)(2,1)S(1)}, bf16[256,4,128]{0,1,2:T(4,128)(2,1)S(1)}, u32[]{:S(2)}, u32[]{:S(2)}) collective-permute-start(bf16[256,4,128]{0,1,2:T(4,128)(2,1)S(1)} %pad_maximum_fusion.4), channel_id=1, source_target_pairs={{0,2},{1,3},{2,0},{3,1},{4,6},{5,7},{6,4},{7,5},{8,10},{9,11},{10,... | collective-permute-start | bytes 786440 | tf_op jit(solution)/shard_map/ppermute | solution.py:21
  122.3 6.8 %collective-permute-done.32 = bf16[256,4,128]{0,1,2:T(4,128)(2,1)S(1)} collective-permute-done((bf16[256,4,128]{0,1,2:T(4,128)(2,1)S(1)}, bf16[256,4,128]{0,1,2:T(4,128)(2,1)S(1)}, u32[]{:S(2)}, u32[]{:S(2)}) %collective-permute-start.32) | collective-permute-done | bytes 262176 | tf_op jit(solution)/shard_map/ppermute | solution.py:21
  129.1 1.7 %fusion.13 = (f32[4,128]{0,1:T(8,128)S(1)}, bf16[512,4,128]{0,1,2:T(4,128)(2,1)S(1)}) fusion(s32[]{:T(128)S(6)} %select_n.97, bf16[256,4,128]{0,1,2:T(4,128)(2,1)S(1)} %collective-permute-done.32, bf16[128,4,128]{0,1,2:T(4,128)(2,1)S(1)} %collective-permute-done.31, bf16[128,4,128]{0,1,2:T(4,128)(2,1)S(1)} %fusion.102), kind=kLoop, calls=%fused_computation.29 | loop fusion | flops 3931648 | bytes 1050628 | tf_op jit(solution)/shard_map/reduce_sum | solution.py:34
  130.9 0.3 fusion.15
  131.3 2.0 %fusion.4 = bf16[512,512]{0,1:T(8,128)(2,1)S(1)} fusion(bf16[512,512]{0,1:T(8,128)(2,1)S(1)} %bitcast.152, bf16[2,512,512]{2,1,0:T(8,128)(2,1)S(1)} %copy-done.3, bf16[2,512,512]{2,1,0:T(8,128)(2,1)} %param.18), kind=kOutput, calls=%fused_computation.19 | convolution fusion | flops 539492352 | bytes 2097152 | tf_op jit(solution)/shard_map/dot_general | solution.py:75
  133.4 1.2 constant_dynamic-slice_fusion.13
  134.9 0.7 collective-permute-start.33
  135.8 1.6 %collective-permute-start.34 = (bf16[128,4,128]{0,1,2:T(4,128)(2,1)S(1)}, bf16[128,4,128]{0,1,2:T(4,128)(2,1)S(1)}, u32[]{:S(2)}, u32[]{:S(2)}) collective-permute-start(bf16[128,4,128]{0,1,2:T(4,128)(2,1)S(1)} %fusion.107), channel_id=1, source_target_pairs={{0,2},{1,3},{2,0},{3,1},{4,6},{5,7},{6,4},{7,5},{8,10},{9,11},{10,... | collective-permute-start | bytes 393224 | tf_op jit(solution)/shard_map/ppermute | solution.py:58
  137.5 1.5 %collective-permute-start.35 = (bf16[128,4,128]{0,1,2:T(4,128)(2,1)S(1)}, bf16[128,4,128]{0,1,2:T(4,128)(2,1)S(1)}, u32[]{:S(2)}, u32[]{:S(2)}) collective-permute-start(bf16[128,4,128]{0,1,2:T(4,128)(2,1)S(1)} %fusion.106), channel_id=1, source_target_pairs={{0,3},{1,0},{2,1},{3,2},{4,7},{5,4},{6,5},{7,6},{8,11},{9,8},{10,9... | collective-permute-start | bytes 393224 | tf_op jit(solution)/shard_map/ppermute | solution.py:58
  139.3 2.3 %collective-permute-done.34 = bf16[128,4,128]{0,1,2:T(4,128)(2,1)S(1)} collective-permute-done((bf16[128,4,128]{0,1,2:T(4,128)(2,1)S(1)}, bf16[128,4,128]{0,1,2:T(4,128)(2,1)S(1)}, u32[]{:S(2)}, u32[]{:S(2)}) %collective-permute-start.34) | collective-permute-done | bytes 131104 | tf_op jit(solution)/shard_map/ppermute | solution.py:58
  141.6 1.5 %collective-permute-done.35 = bf16[128,4,128]{0,1,2:T(4,128)(2,1)S(1)} collective-permute-done((bf16[128,4,128]{0,1,2:T(4,128)(2,1)S(1)}, bf16[128,4,128]{0,1,2:T(4,128)(2,1)S(1)}, u32[]{:S(2)}, u32[]{:S(2)}) %collective-permute-start.35) | collective-permute-done | bytes 131104 | tf_op jit(solution)/shard_map/ppermute | solution.py:58
  143.2 0.3 add_convert_fusion
  143.5 0.8 copy.170
  (90 shorter events, 5.5 us)
Async XLA Ops:
  0.0 24.6 %copy-start = (bf16[3,128,512]{2,1,0:T(8,128)(2,1)S(1)}, bf16[3,128,512]{2,1,0:T(8,128)(2,1)}, u32[]{:S(2)}) copy-start(bf16[3,128,512]{2,1,0:T(8,128)(2,1)} %param.14) | copy-start | bytes 1179652
  0.0 5.2 %collective-permute-start = (bf16[128,4,128]{2,1,0:T(4,128)(2,1)}, bf16[128,4,128]{2,1,0:T(4,128)(2,1)S(1)}, u32[]{:S(2)}, u32[]{:S(2)}) collective-permute-start(bf16[128,4,128]{2,1,0:T(4,128)(2,1)} %param.12), channel_id=1, source_target_pairs={{0,3},{1,0},{2,1},{3,2},{4,7},{5,4},{6,5},{7,6},{8,11},{9,8},{10,9... | collective-permute-start | bytes 393224 | tf_op jit(solution)/shard_map/ppermute | solution.py:21
  3.5 56.7 %collective-permute-start.8 = (bf16[128,4,1]{0,1,2:T(4,128)(2,1)S(1)}, bf16[128,4,1]{0,1,2:T(4,128)(2,1)S(1)}, u32[]{:S(2)}, u32[]{:S(2)}) collective-permute-start(bf16[128,4,1]{0,1,2:T(4,128)(2,1)S(1)} %get-tuple-element.49), channel_id=1, source_target_pairs={{0,4},{4,8},{8,12},{12,0},{1,5},{5,9},{9,13},{13,1},{2,6},{6,10},{... | collective-permute-start | bytes 3080 | tf_op jit(solution)/shard_map/ppermute | solution.py:158
  6.3 9.0 %collective-permute-start.1 = (bf16[256,4,128]{2,1,0:T(4,128)(2,1)S(1)}, bf16[256,4,128]{2,1,0:T(4,128)(2,1)S(1)}, u32[]{:S(2)}, u32[]{:S(2)}) collective-permute-start(bf16[256,4,128]{2,1,0:T(4,128)(2,1)S(1)} %pad_maximum_fusion.1), channel_id=1, source_target_pairs={{0,2},{1,3},{2,0},{3,1},{4,6},{5,7},{6,4},{7,5},{8,10},{9,11},{10,... | collective-permute-start | bytes 786440 | tf_op jit(solution)/shard_map/ppermute | solution.py:21
  25.2 11.2 %collective-permute-start.2 = (bf16[2,2,64,4,128]{4,2,3,1,0:T(8,128)(2,1)S(1)}, bf16[2,2,64,4,128]{4,2,3,1,0:T(8,128)(2,1)S(1)}, u32[]{:S(2)}, u32[]{:S(2)}) collective-permute-start(bf16[2,2,64,4,128]{4,2,3,1,0:T(8,128)(2,1)S(1)} %pad_maximum_fusion.2), channel_id=1, source_target_pairs={{0,4},{4,8},{8,12},{12,0},{1,5},{5,9},{9,13},{13,1},{2,6},{6,10},{... | collective-permute-start | bytes 786440 | tf_op jit(solution)/shard_map/ppermute | solution.py:90
  26.8 19.7 %collective-permute-start.3 = (bf16[2,2,64,4,128]{4,2,3,1,0:T(8,128)(2,1)S(1)}, bf16[2,2,64,4,128]{4,2,3,1,0:T(8,128)(2,1)S(1)}, u32[]{:S(2)}, u32[]{:S(2)}) collective-permute-start(bf16[2,2,64,4,128]{4,2,3,1,0:T(8,128)(2,1)S(1)} %pad_maximum_fusion.2), channel_id=1, source_target_pairs={{0,8},{4,12},{8,0},{12,4},{1,9},{5,13},{9,1},{13,5},{2,10},{6,14},... | collective-permute-start | bytes 786440 | tf_op jit(solution)/shard_map/ppermute | solution.py:90
  29.4 17.1 %collective-permute-start.4 = (bf16[2,2,64,4,128]{4,2,3,1,0:T(8,128)(2,1)S(1)}, bf16[2,2,64,4,128]{4,2,3,1,0:T(8,128)(2,1)S(1)}, u32[]{:S(2)}, u32[]{:S(2)}) collective-permute-start(bf16[2,2,64,4,128]{4,2,3,1,0:T(8,128)(2,1)S(1)} %pad_maximum_fusion.2), channel_id=1, source_target_pairs={{0,12},{4,0},{8,4},{12,8},{1,13},{5,1},{9,5},{13,9},{2,14},{6,2},{... | collective-permute-start | bytes 786440 | tf_op jit(solution)/shard_map/ppermute | solution.py:90
  47.3 0.9 copy-start.1
  50.4 13.6 %collective-permute-start.9 = (bf16[128,4,1]{0,1,2:T(4,128)(2,1)S(1)}, bf16[128,4,1]{0,1,2:T(4,128)(2,1)S(1)}, u32[]{:S(2)}, u32[]{:S(2)}) collective-permute-start(bf16[128,4,1]{0,1,2:T(4,128)(2,1)S(1)} %get-tuple-element.51), channel_id=1, source_target_pairs={{0,4},{1,5},{2,6},{3,7},{4,8},{5,9},{6,10},{7,11},{8,12},{9,13},{1... | collective-permute-start | bytes 3080 | tf_op jit(solution)/shard_map/ppermute | solution.py:66
  56.6 27.1 %copy-start.2 = (f32[2,512]{1,0:T(2,128)S(1)}, f32[2,512]{1,0:T(2,128)}, u32[]{:S(2)}) copy-start(f32[2,512]{1,0:T(2,128)} %param.17) | copy-start | bytes 12292
  56.8 7.3 %collective-permute-start.10 = (bf16[128,4,1]{0,1,2:T(4,128)(2,1)S(1)}, bf16[128,4,1]{0,1,2:T(4,128)(2,1)S(1)}, u32[]{:S(2)}, u32[]{:S(2)}) collective-permute-start(bf16[128,4,1]{0,1,2:T(4,128)(2,1)S(1)} %get-tuple-element.53), channel_id=1, source_target_pairs={{0,5},{1,6},{2,7},{3,4},{4,9},{5,10},{6,11},{7,8},{8,13},{9,14},{1... | collective-permute-start | bytes 3080 | tf_op jit(solution)/shard_map/ppermute | solution.py:66
  57.1 7.1 %collective-permute-start.11 = (bf16[128,4,1]{0,1,2:T(4,128)(2,1)S(1)}, bf16[128,4,1]{0,1,2:T(4,128)(2,1)S(1)}, u32[]{:S(2)}, u32[]{:S(2)}) collective-permute-start(bf16[128,4,1]{0,1,2:T(4,128)(2,1)S(1)} %get-tuple-element.55), channel_id=1, source_target_pairs={{0,6},{1,7},{2,4},{3,5},{4,10},{5,11},{6,8},{7,9},{8,14},{9,15},{1... | collective-permute-start | bytes 3080 | tf_op jit(solution)/shard_map/ppermute | solution.py:66
  58.6 8.1 %collective-permute-start.12 = (bf16[128,4,1]{0,1,2:T(4,128)(2,1)S(1)}, bf16[128,4,1]{0,1,2:T(4,128)(2,1)S(1)}, u32[]{:S(2)}, u32[]{:S(2)}) collective-permute-start(bf16[128,4,1]{0,1,2:T(4,128)(2,1)S(1)} %get-tuple-element.57), channel_id=1, source_target_pairs={{0,7},{1,4},{2,5},{3,6},{4,11},{5,8},{6,9},{7,10},{8,15},{9,12},{1... | collective-permute-start | bytes 3080 | tf_op jit(solution)/shard_map/ppermute | solution.py:66
  60.2 9.8 %collective-permute-start.13 = (bf16[128,4,1]{0,1,2:T(4,128)(2,1)S(1)}, bf16[128,4,1]{0,1,2:T(4,128)(2,1)S(1)}, u32[]{:S(2)}, u32[]{:S(2)}) collective-permute-start(bf16[128,4,1]{0,1,2:T(4,128)(2,1)S(1)} %get-tuple-element.50), channel_id=1, source_target_pairs={{0,12},{4,0},{8,4},{12,8},{1,13},{5,1},{9,5},{13,9},{2,14},{6,2},{... | collective-permute-start | bytes 3080 | tf_op jit(solution)/shard_map/ppermute | solution.py:161
  64.0 6.0 %collective-permute-start.14 = (bf16[128,4,1]{0,1,2:T(4,128)(2,1)S(1)}, bf16[128,4,1]{0,1,2:T(4,128)(2,1)S(1)}, u32[]{:S(2)}, u32[]{:S(2)}) collective-permute-start(bf16[128,4,1]{0,1,2:T(4,128)(2,1)S(1)} %get-tuple-element.52), channel_id=1, source_target_pairs={{0,12},{1,13},{2,14},{3,15},{4,0},{5,1},{6,2},{7,3},{8,4},{9,5},{1... | collective-permute-start | bytes 3080 | tf_op jit(solution)/shard_map/ppermute | solution.py:66
  64.1 6.8 %collective-permute-start.15 = (bf16[128,4,1]{0,1,2:T(4,128)(2,1)S(1)}, bf16[128,4,1]{0,1,2:T(4,128)(2,1)S(1)}, u32[]{:S(2)}, u32[]{:S(2)}) collective-permute-start(bf16[128,4,1]{0,1,2:T(4,128)(2,1)S(1)} %get-tuple-element.54), channel_id=1, source_target_pairs={{0,13},{1,14},{2,15},{3,12},{4,1},{5,2},{6,3},{7,0},{8,5},{9,6},{1... | collective-permute-start | bytes 3080 | tf_op jit(solution)/shard_map/ppermute | solution.py:66
  64.1 8.2 %collective-permute-start.16 = (bf16[128,4,1]{0,1,2:T(4,128)(2,1)S(1)}, bf16[128,4,1]{0,1,2:T(4,128)(2,1)S(1)}, u32[]{:S(2)}, u32[]{:S(2)}) collective-permute-start(bf16[128,4,1]{0,1,2:T(4,128)(2,1)S(1)} %get-tuple-element.56), channel_id=1, source_target_pairs={{0,14},{1,15},{2,12},{3,13},{4,2},{5,3},{6,0},{7,1},{8,6},{9,7},{1... | collective-permute-start | bytes 3080 | tf_op jit(solution)/shard_map/ppermute | solution.py:66
  66.6 5.7 %collective-permute-start.17 = (bf16[128,4,1]{0,1,2:T(4,128)(2,1)S(1)}, bf16[128,4,1]{0,1,2:T(4,128)(2,1)S(1)}, u32[]{:S(2)}, u32[]{:S(2)}) collective-permute-start(bf16[128,4,1]{0,1,2:T(4,128)(2,1)S(1)} %get-tuple-element.58), channel_id=1, source_target_pairs={{0,15},{1,12},{2,13},{3,14},{4,3},{5,0},{6,1},{7,2},{8,7},{9,4},{1... | collective-permute-start | bytes 3080 | tf_op jit(solution)/shard_map/ppermute | solution.py:66
  70.0 5.2 %collective-permute-start.5 = (bf16[128,4,128]{0,1,2:T(4,128)(2,1)S(1)}, bf16[128,4,128]{0,1,2:T(4,128)(2,1)S(1)}, u32[]{:S(2)}, u32[]{:S(2)}) collective-permute-start(bf16[128,4,128]{0,1,2:T(4,128)(2,1)S(1)} %fusion.118), channel_id=1, source_target_pairs={{0,1},{1,2},{2,3},{3,0},{4,5},{5,6},{6,7},{7,4},{8,9},{9,10},{10,1... | collective-permute-start | bytes 393224 | tf_op jit(solution)/shard_map/ppermute | solution.py:58
  70.0 6.4 %collective-permute-start.6 = (bf16[128,4,128]{0,1,2:T(4,128)(2,1)S(1)}, bf16[128,4,128]{0,1,2:T(4,128)(2,1)S(1)}, u32[]{:S(2)}, u32[]{:S(2)}) collective-permute-start(bf16[128,4,128]{0,1,2:T(4,128)(2,1)S(1)} %fusion.117), channel_id=1, source_target_pairs={{0,2},{1,3},{2,0},{3,1},{4,6},{5,7},{6,4},{7,5},{8,10},{9,11},{10,... | collective-permute-start | bytes 393224 | tf_op jit(solution)/shard_map/ppermute | solution.py:58
  70.9 6.0 %collective-permute-start.7 = (bf16[128,4,128]{0,1,2:T(4,128)(2,1)S(1)}, bf16[128,4,128]{0,1,2:T(4,128)(2,1)S(1)}, u32[]{:S(2)}, u32[]{:S(2)}) collective-permute-start(bf16[128,4,128]{0,1,2:T(4,128)(2,1)S(1)} %fusion.116), channel_id=1, source_target_pairs={{0,3},{1,0},{2,1},{3,2},{4,7},{5,4},{6,5},{7,6},{8,11},{9,8},{10,9... | collective-permute-start | bytes 393224 | tf_op jit(solution)/shard_map/ppermute | solution.py:58
  77.8 15.7 %copy-start.3 = (bf16[2,512,512]{2,1,0:T(8,128)(2,1)S(1)}, bf16[2,512,512]{2,1,0:T(8,128)(2,1)}, u32[]{:S(2)}) copy-start(bf16[2,512,512]{2,1,0:T(8,128)(2,1)} %param.19) | copy-start | bytes 3145732
  77.8 4.5 %collective-permute-start.18 = (bf16[128,4,128]{0,1,2:T(4,128)(2,1)S(1)}, bf16[128,4,128]{0,1,2:T(4,128)(2,1)S(1)}, u32[]{:S(2)}, u32[]{:S(2)}) collective-permute-start(bf16[128,4,128]{0,1,2:T(4,128)(2,1)S(1)} %fusion.103), channel_id=1, source_target_pairs={{0,3},{1,0},{2,1},{3,2},{4,7},{5,4},{6,5},{7,6},{8,11},{9,8},{10,9... | collective-permute-start | bytes 393224 | tf_op jit(solution)/shard_map/ppermute | solution.py:21
  82.4 8.8 %collective-permute-start.19 = (bf16[256,4,128]{0,1,2:T(4,128)(2,1)S(1)}, bf16[256,4,128]{0,1,2:T(4,128)(2,1)S(1)}, u32[]{:S(2)}, u32[]{:S(2)}) collective-permute-start(bf16[256,4,128]{0,1,2:T(4,128)(2,1)S(1)} %pad_maximum_fusion.3), channel_id=1, source_target_pairs={{0,2},{1,3},{2,0},{3,1},{4,6},{5,7},{6,4},{7,5},{8,10},{9,11},{10,... | collective-permute-start | bytes 786440 | tf_op jit(solution)/shard_map/ppermute | solution.py:21
  97.3 7.1 %collective-permute-start.23 = (bf16[128,4,1]{0,1,2:T(4,128)(2,1)S(1)}, bf16[128,4,1]{0,1,2:T(4,128)(2,1)S(1)}, u32[]{:S(2)}, u32[]{:S(2)}) collective-permute-start(bf16[128,4,1]{0,1,2:T(4,128)(2,1)S(1)} %get-tuple-element.41), channel_id=1, source_target_pairs={{0,4},{1,5},{2,6},{3,7},{4,8},{5,9},{6,10},{7,11},{8,12},{9,13},{1... | collective-permute-start | bytes 3080 | tf_op jit(solution)/shard_map/ppermute | solution.py:66
  97.6 6.9 %collective-permute-start.24 = (bf16[128,4,1]{0,1,2:T(4,128)(2,1)S(1)}, bf16[128,4,1]{0,1,2:T(4,128)(2,1)S(1)}, u32[]{:S(2)}, u32[]{:S(2)}) collective-permute-start(bf16[128,4,1]{0,1,2:T(4,128)(2,1)S(1)} %get-tuple-element.43), channel_id=1, source_target_pairs={{0,5},{1,6},{2,7},{3,4},{4,9},{5,10},{6,11},{7,8},{8,13},{9,14},{1... | collective-permute-start | bytes 3080 | tf_op jit(solution)/shard_map/ppermute | solution.py:66
  98.4 7.8 %collective-permute-start.25 = (bf16[128,4,1]{0,1,2:T(4,128)(2,1)S(1)}, bf16[128,4,1]{0,1,2:T(4,128)(2,1)S(1)}, u32[]{:S(2)}, u32[]{:S(2)}) collective-permute-start(bf16[128,4,1]{0,1,2:T(4,128)(2,1)S(1)} %get-tuple-element.45), channel_id=1, source_target_pairs={{0,6},{1,7},{2,4},{3,5},{4,10},{5,11},{6,8},{7,9},{8,14},{9,15},{1... | collective-permute-start | bytes 3080 | tf_op jit(solution)/shard_map/ppermute | solution.py:66
  100.1 8.2 %collective-permute-start.26 = (bf16[128,4,1]{0,1,2:T(4,128)(2,1)S(1)}, bf16[128,4,1]{0,1,2:T(4,128)(2,1)S(1)}, u32[]{:S(2)}, u32[]{:S(2)}) collective-permute-start(bf16[128,4,1]{0,1,2:T(4,128)(2,1)S(1)} %get-tuple-element.47), channel_id=1, source_target_pairs={{0,7},{1,4},{2,5},{3,6},{4,11},{5,8},{6,9},{7,10},{8,15},{9,12},{1... | collective-permute-start | bytes 3080 | tf_op jit(solution)/shard_map/ppermute | solution.py:66
  104.4 7.4 %collective-permute-start.20 = (bf16[128,4,128]{0,1,2:T(4,128)(2,1)S(1)}, bf16[128,4,128]{0,1,2:T(4,128)(2,1)S(1)}, u32[]{:S(2)}, u32[]{:S(2)}) collective-permute-start(bf16[128,4,128]{0,1,2:T(4,128)(2,1)S(1)} %fusion.113), channel_id=1, source_target_pairs={{0,1},{1,2},{2,3},{3,0},{4,5},{5,6},{6,7},{7,4},{8,9},{9,10},{10,1... | collective-permute-start | bytes 393224 | tf_op jit(solution)/shard_map/ppermute | solution.py:58
  104.4 5.2 %collective-permute-start.27 = (bf16[128,4,1]{0,1,2:T(4,128)(2,1)S(1)}, bf16[128,4,1]{0,1,2:T(4,128)(2,1)S(1)}, u32[]{:S(2)}, u32[]{:S(2)}) collective-permute-start(bf16[128,4,1]{0,1,2:T(4,128)(2,1)S(1)} %get-tuple-element.42), channel_id=1, source_target_pairs={{0,12},{1,13},{2,14},{3,15},{4,0},{5,1},{6,2},{7,3},{8,4},{9,5},{1... | collective-permute-start | bytes 3080 | tf_op jit(solution)/shard_map/ppermute | solution.py:66
  104.5 6.7 %collective-permute-start.28 = (bf16[128,4,1]{0,1,2:T(4,128)(2,1)S(1)}, bf16[128,4,1]{0,1,2:T(4,128)(2,1)S(1)}, u32[]{:S(2)}, u32[]{:S(2)}) collective-permute-start(bf16[128,4,1]{0,1,2:T(4,128)(2,1)S(1)} %get-tuple-element.44), channel_id=1, source_target_pairs={{0,13},{1,14},{2,15},{3,12},{4,1},{5,2},{6,3},{7,0},{8,5},{9,6},{1... | collective-permute-start | bytes 3080 | tf_op jit(solution)/shard_map/ppermute | solution.py:66
  106.2 5.6 %collective-permute-start.29 = (bf16[128,4,1]{0,1,2:T(4,128)(2,1)S(1)}, bf16[128,4,1]{0,1,2:T(4,128)(2,1)S(1)}, u32[]{:S(2)}, u32[]{:S(2)}) collective-permute-start(bf16[128,4,1]{0,1,2:T(4,128)(2,1)S(1)} %get-tuple-element.46), channel_id=1, source_target_pairs={{0,14},{1,15},{2,12},{3,13},{4,2},{5,3},{6,0},{7,1},{8,6},{9,7},{1... | collective-permute-start | bytes 3080 | tf_op jit(solution)/shard_map/ppermute | solution.py:66
  108.3 3.6 %collective-permute-start.30 = (bf16[128,4,1]{0,1,2:T(4,128)(2,1)S(1)}, bf16[128,4,1]{0,1,2:T(4,128)(2,1)S(1)}, u32[]{:S(2)}, u32[]{:S(2)}) collective-permute-start(bf16[128,4,1]{0,1,2:T(4,128)(2,1)S(1)} %get-tuple-element.48), channel_id=1, source_target_pairs={{0,15},{1,12},{2,13},{3,14},{4,3},{5,0},{6,1},{7,2},{8,7},{9,4},{1... | collective-permute-start | bytes 3080 | tf_op jit(solution)/shard_map/ppermute | solution.py:66
  109.6 6.3 %collective-permute-start.21 = (bf16[128,4,128]{0,1,2:T(4,128)(2,1)S(1)}, bf16[128,4,128]{0,1,2:T(4,128)(2,1)S(1)}, u32[]{:S(2)}, u32[]{:S(2)}) collective-permute-start(bf16[128,4,128]{0,1,2:T(4,128)(2,1)S(1)} %fusion.112), channel_id=1, source_target_pairs={{0,2},{1,3},{2,0},{3,1},{4,6},{5,7},{6,4},{7,5},{8,10},{9,11},{10,... | collective-permute-start | bytes 393224 | tf_op jit(solution)/shard_map/ppermute | solution.py:58
  111.3 4.6 %collective-permute-start.22 = (bf16[128,4,128]{0,1,2:T(4,128)(2,1)S(1)}, bf16[128,4,128]{0,1,2:T(4,128)(2,1)S(1)}, u32[]{:S(2)}, u32[]{:S(2)}) collective-permute-start(bf16[128,4,128]{0,1,2:T(4,128)(2,1)S(1)} %fusion.111), channel_id=1, source_target_pairs={{0,3},{1,0},{2,1},{3,2},{4,7},{5,4},{6,5},{7,6},{8,11},{9,8},{10,9... | collective-permute-start | bytes 393224 | tf_op jit(solution)/shard_map/ppermute | solution.py:58
  116.7 3.8 %collective-permute-start.31 = (bf16[128,4,128]{0,1,2:T(4,128)(2,1)S(1)}, bf16[128,4,128]{0,1,2:T(4,128)(2,1)S(1)}, u32[]{:S(2)}, u32[]{:S(2)}) collective-permute-start(bf16[128,4,128]{0,1,2:T(4,128)(2,1)S(1)} %fusion.102), channel_id=1, source_target_pairs={{0,3},{1,0},{2,1},{3,2},{4,7},{5,4},{6,5},{7,6},{8,11},{9,8},{10,9... | collective-permute-start | bytes 393224 | tf_op jit(solution)/shard_map/ppermute | solution.py:21
  120.7 8.4 %collective-permute-start.32 = (bf16[256,4,128]{0,1,2:T(4,128)(2,1)S(1)}, bf16[256,4,128]{0,1,2:T(4,128)(2,1)S(1)}, u32[]{:S(2)}, u32[]{:S(2)}) collective-permute-start(bf16[256,4,128]{0,1,2:T(4,128)(2,1)S(1)} %pad_maximum_fusion.4), channel_id=1, source_target_pairs={{0,2},{1,3},{2,0},{3,1},{4,6},{5,7},{6,4},{7,5},{8,10},{9,11},{10,... | collective-permute-start | bytes 786440 | tf_op jit(solution)/shard_map/ppermute | solution.py:21
  134.9 4.4 %collective-permute-start.33 = (bf16[128,4,128]{0,1,2:T(4,128)(2,1)S(1)}, bf16[128,4,128]{0,1,2:T(4,128)(2,1)S(1)}, u32[]{:S(2)}, u32[]{:S(2)}) collective-permute-start(bf16[128,4,128]{0,1,2:T(4,128)(2,1)S(1)} %fusion.108), channel_id=1, source_target_pairs={{0,1},{1,2},{2,3},{3,0},{4,5},{5,6},{6,7},{7,4},{8,9},{9,10},{10,1... | collective-permute-start | bytes 393224 | tf_op jit(solution)/shard_map/ppermute | solution.py:58
  135.8 5.9 %collective-permute-start.34 = (bf16[128,4,128]{0,1,2:T(4,128)(2,1)S(1)}, bf16[128,4,128]{0,1,2:T(4,128)(2,1)S(1)}, u32[]{:S(2)}, u32[]{:S(2)}) collective-permute-start(bf16[128,4,128]{0,1,2:T(4,128)(2,1)S(1)} %fusion.107), channel_id=1, source_target_pairs={{0,2},{1,3},{2,0},{3,1},{4,6},{5,7},{6,4},{7,5},{8,10},{9,11},{10,... | collective-permute-start | bytes 393224 | tf_op jit(solution)/shard_map/ppermute | solution.py:58
  137.5 5.7 %collective-permute-start.35 = (bf16[128,4,128]{0,1,2:T(4,128)(2,1)S(1)}, bf16[128,4,128]{0,1,2:T(4,128)(2,1)S(1)}, u32[]{:S(2)}, u32[]{:S(2)}) collective-permute-start(bf16[128,4,128]{0,1,2:T(4,128)(2,1)S(1)} %fusion.106), channel_id=1, source_target_pairs={{0,3},{1,0},{2,1},{3,2},{4,7},{5,4},{6,5},{7,6},{8,11},{9,8},{10,9... | collective-permute-start | bytes 393224 | tf_op jit(solution)/shard_map/ppermute | solution.py:58
